TPU v7x, 512 devices: a whole 4x4x16 slice. The times are simulated.
512 devices in a mesh: pipe: 16 (over z_hi, x, core), tensor: 32 (over z_lo, y).
Axes of the slice: x: 4, y: 4, z: 16 (z_hi: 2, z_lo: 8; z = z_hi * 8 + z_lo), core: 2. Of those that a mesh axis runs over, the one named last changes fastest.
Arguments:
- tokens: bfloat16 [512, 8192], P(None, 'pipe'), may hold values from -6 to 6
- out_grad: bfloat16 [512, 8192], P(None, 'pipe'), may hold values from -6 to 6
- w_gate: bfloat16 [8192, 16384], P('pipe', 'tensor'), may hold values from -0.0625 to 0.0625
- w_up: bfloat16 [8192, 16384], P('pipe', 'tensor'), may hold values from -0.0625 to 0.0625
- w_down: bfloat16 [16384, 8192], P('tensor', 'pipe'), may hold values from -0.046875 to 0.046875
Outputs:
- input_grad: float32 [512, 8192], P('tensor', 'pipe')
- gate_mantissa: bfloat16 [8192, 16384], P('pipe', 'tensor')
- gate_scales: float32 [256, 8192], P('pipe', 'tensor')
- up_mantissa: bfloat16 [8192, 16384], P('pipe', 'tensor')
- up_scales: float32 [256, 8192], P('pipe', 'tensor')
- down_mantissa: bfloat16 [16384, 8192], P('tensor', 'pipe')
- down_scales: float32 [8192, 256], P('tensor', 'pipe')
All inputs are finite; a program needn't handle non-finite values.
Results may differ from a plain program's by a relative error of at most 0.0049.
Values may be sent and summed in bfloat16 or wider, within the bound.
No kernel may reach another device: no remote copies, remote signals or barrier semaphores. Data moves between devices by JAX's collectives and lax.ppermute only.
A program may use at most 64 MiB of HBM per device.

v0:
```python
import jax
import jax.numpy as jnp
from jax import lax
from jax.sharding import PartitionSpec as P


def quantize_features(grad):
    mags = jnp.abs(grad)
    paired = jnp.maximum(mags[:, 0::2], mags[:, 1::2])
    scales = jnp.max(paired.reshape(paired.shape[0] // 32, 32, paired.shape[1]), axis=1) + 1e-06
    spread = jnp.repeat(scales, 2, axis=1)
    mantissa = (grad.reshape(grad.shape[0] // 32, 32, grad.shape[1]) / spread[:, None, :]).reshape(
        grad.shape
    )
    return (mantissa.astype(jnp.bfloat16), scales)


def quantize_hidden(grad):
    mags = jnp.abs(grad)
    paired = jnp.maximum(mags[0::2], mags[1::2])
    scales = jnp.max(paired.reshape(paired.shape[0], paired.shape[1] // 32, 32), axis=2) + 1e-06
    spread = jnp.repeat(scales, 32, axis=1)
    mantissa = (grad.reshape(grad.shape[0] // 2, 2, grad.shape[1]) / spread[:, None, :]).reshape(
        grad.shape
    )
    return (mantissa.astype(jnp.bfloat16), scales)


def contract_last(left, right):
    return lax.dot_general(
        left, right, (((1,), (1,)), ((), ())), preferred_element_type=jnp.float32
    )


def contract_first(left, right):
    return lax.dot_general(
        left, right, (((0,), (0,)), ((), ())), preferred_element_type=jnp.float32
    )


def gate_terms(gate, up, hidden_grad):
    sigmoid_gate = jax.nn.sigmoid(gate)
    silu_gate = gate * sigmoid_gate
    hidden = (silu_gate * up).astype(jnp.bfloat16)
    gate_grad = (hidden_grad * up * sigmoid_gate * (1.0 + gate * (1.0 - sigmoid_gate))).astype(
        jnp.bfloat16
    )
    up_grad = (hidden_grad * silu_gate).astype(jnp.bfloat16)
    return (hidden, gate_grad, up_grad)


def on_device(tokens, out_grad, w_gate, w_up, w_down):
    gate_part = jnp.dot(tokens, w_gate, preferred_element_type=jnp.float32)
    up_part = jnp.dot(tokens, w_up, preferred_element_type=jnp.float32)
    hidden_part = contract_last(out_grad, w_down)
    gate, up, hidden_grad = lax.psum((gate_part, up_part, hidden_part), "pipe")
    hidden, gate_grad, up_grad = gate_terms(gate, up, hidden_grad)
    input_grad = lax.psum_scatter(
        contract_last(gate_grad, w_gate) + contract_last(up_grad, w_up),
        "tensor",
        scatter_dimension=0,
        tiled=True,
    )
    gate_mantissa, gate_scales = quantize_features(contract_first(tokens, gate_grad))
    up_mantissa, up_scales = quantize_features(contract_first(tokens, up_grad))
    down_mantissa, down_scales = quantize_hidden(contract_first(hidden, out_grad))
    return (
        input_grad,
        gate_mantissa,
        gate_scales,
        up_mantissa,
        up_scales,
        down_mantissa,
        down_scales,
    )


def solution(mesh):
    in_specs = (
        P(None, "pipe"),
        P(None, "pipe"),
        P("pipe", "tensor"),
        P("pipe", "tensor"),
        P("tensor", "pipe"),
    )
    out_specs = (
        P("tensor", "pipe"),
        P("pipe", "tensor"),
        P("pipe", "tensor"),
        P("pipe", "tensor"),
        P("pipe", "tensor"),
        P("tensor", "pipe"),
        P("tensor", "pipe"),
    )
    return jax.shard_map(
        on_device, mesh=mesh, in_specs=in_specs, out_specs=out_specs, check_vma=False
    )
```

profile of v0, /device:TPU:6, one launch (start us, length us, event | category | flops | bytes accessed | tf_op | source)
XLA Modules:
  0.0 568.2 jit_solution(10124648394877445380)
XLA Ops:
  7.2 1.0 copy-done
  8.2 2.5 fusion.11
  10.7 1.4 fusion.10
  12.1 1.4 fusion.9
  13.6 292.7 %all-reduce.3.cloned.1.call-done = (f32[512,512]{1,0:T(8,128)}, f32[512,512]{1,0:T(8,128)}, f32[512,512]{1,0:T(8,128)}) async-done(((f32[512,512]{1,0:T(8,128)}, f32[512,512]{1,0:T(8,128)}, f32[512,512]{1,0:T(8,128)}), (f32[512,512]{1,0:T(8,128)}, f32[512,512]{1,0:T(8,128)}, f32[512,512]{1,0:T(8,128)})) %all-reduce.3.cloned.1.call-update) | async-done | bytes 3145744 | tf_op jit(solution)/shard_map/psum | solution.py:56
  306.4 2.5 multiply_convert_fusion.1
  308.9 0.5 fusion.12
  309.4 1.4 convolution_add_fusion
  310.8 3.2 fusion.8
  314.0 19.9 %slice.23 = f32[256,512]{0,1:T(8,128)} slice(f32[512,512]{0,1:T(8,128)S(1)} %get-tuple-element.37), slice={[1:512:2], [0:512:1]} | slice | bytes 1048576 | tf_op jit(solution)/shard_map/slice | solution.py:20
  333.9 19.9 %slice.22 = f32[256,512]{0,1:T(8,128)} slice(f32[512,512]{0,1:T(8,128)S(1)} %get-tuple-element.37), slice={[0:512:2], [0:512:1]} | slice | bytes 1048576 | tf_op jit(solution)/shard_map/slice | solution.py:20
  353.9 1.5 fusion.7
  355.3 20.8 %slice.21 = f32[512,256]{1,0:T(8,128)} slice(f32[512,512]{1,0:T(8,128)} %get-tuple-element.35), slice={[0:512:1], [1:512:2]} | slice | bytes 1048576 | tf_op jit(solution)/shard_map/slice | solution.py:9
  376.1 19.9 %slice.20 = f32[512,256]{1,0:T(8,128)} slice(f32[512,512]{1,0:T(8,128)S(1)} %copy-done.2), slice={[0:512:1], [0:512:2]} | slice | bytes 1048576 | tf_op jit(solution)/shard_map/slice | solution.py:9
  396.0 1.5 fusion.6
  397.5 19.9 %slice.19 = f32[512,256]{1,0:T(8,128)} slice(f32[512,512]{1,0:T(8,128)S(1)} %get-tuple-element.33), slice={[0:512:1], [1:512:2]} | slice | bytes 1048576 | tf_op jit(solution)/shard_map/slice | solution.py:9
  417.4 19.9 %slice.18 = f32[512,256]{1,0:T(8,128)} slice(f32[512,512]{1,0:T(8,128)S(1)} %get-tuple-element.33), slice={[0:512:1], [0:512:2]} | slice | bytes 1048576 | tf_op jit(solution)/shard_map/slice | solution.py:9
  437.3 1.1 bitcast_reduce_fusion
  438.6 0.6 copy-done.11
  439.1 0.2 copy.24
  439.3 0.4 div.52
  439.7 1.7 div.53
  441.4 1.6 copy.25
  443.0 1.4 divide_convert_fusion
  444.4 1.0 copy.26
  445.4 0.3 copy-done.5
  446.0 0.5 copy-done.12
  446.7 0.2 copy-done.3
  446.9 1.1 bitcast_reduce_fusion.2
  448.2 0.5 copy-done.13
  448.9 1.2 fusion
  450.1 111.3 %reduce-scatter.2.cloned.1.call-done = f32[16,512]{1,0:T(8,128)} async-done(((f32[512,512]{1,0:T(8,128)}), f32[16,512]{1,0:T(8,128)}) %reduce-scatter.2.cloned.1.call-update) | async-done | bytes 32784 | tf_op jit(solution)/shard_map/reduce_scatter | solution.py:58
  (37 shorter events, 0.9 us)
Async XLA Ops:
  7.2 1.0 copy-start
  7.2 3.5 copy-start.8
  7.2 299.2 %all-reduce.3.cloned.1.call-start = ((), (), s32[]{:S(2)}) async-start(), calls=%async_computation.2 | async-start | bytes 6291456 | tf_op jit(solution)/shard_map/psum | solution.py:56
  10.7 1.4 copy-start.9
  10.7 1.4 copy-start.10
  13.6 547.7 %reduce-scatter.2.cloned.1.call-start = ((), (), s32[]{:S(2)}) async-start(), calls=%async_computation.1 | async-start | bytes 1081344 | tf_op jit(solution)/shard_map/reduce_scatter | solution.py:58
  306.4 2.5 copy-start.7
  355.3 20.8 %copy-start.2 = (f32[512,512]{1,0:T(8,128)S(1)}, f32[512,512]{1,0:T(8,128)}, u32[]{:S(2)}) copy-start(f32[512,512]{1,0:T(8,128)} %get-tuple-element.35) | copy-start | bytes 3145732
  417.4 19.9 %copy-start.6 = (f32[256,512]{0,1:T(8,128)S(1)}, f32[256,512]{0,1:T(8,128)}, u32[]{:S(2)}) copy-start(f32[256,512]{0,1:T(8,128)} %slice.23) | copy-start | bytes 1572868
  438.5 0.6 copy-start.11
  444.4 1.0 copy-start.4
  444.4 1.4 copy-start.5
  445.9 1.1 copy-start.3
  445.9 0.6 copy-start.12
  446.6 2.3 copy-start.1
  448.1 0.6 copy-start.13
Sparse Core Ops, SparseCore 0:
  13.7 292.6 all-reduce.2
  311.0 250.3 reduce-scatter.1
where the time goes:
time: 569 us; the launch traced here: 568 us
  waiting for transfers between devices  404 us (71%)
  local copies, waits for them, and re-layouts  129 us (23%)
  between operations  14.2 us (2%)
  matrix products  13.3 us (2%)
  other arithmetic  7.52 us (1%)
    psum x1, waiting for transfers between devices, on_device(): gate, up, hidden_grad = lax.psum((gate_part, up_part, hidden_part), 'pipe')  293 us
    reduce_scatter x1, waiting for transfers between devices, on_device(): lax.psum_scatter(contract_last(gate_grad, w_gate) + contract_last(up_grad...  111 us
    slice x4, local copies, waits for them, and re-layouts, quantize_features(): paired = jnp.maximum(mags[:, 0::2], mags[:, 1::2])  80.6 us
    slice x2, local copies, waits for them, and re-layouts, quantize_hidden(): paired = jnp.maximum(mags[0::2], mags[1::2])  39.9 us
  transfers between devices with their start and end apart: 2, of which 2 were waited for; matrix products, arithmetic and copies ran while one was open for 24% of the time, Pallas kernels for 0%

commit v1 on v0

v1 whole, which is shorter than its diff:
```python
import jax
import jax.numpy as jnp
import numpy as np
from jax import lax
from jax.sharding import Mesh
from jax.sharding import PartitionSpec as P

PIPE_MODE = "hier"
TENSOR_MODE = "zlo_y"

PIPE = ("z_hi", "x", "core")
TENSOR = ("z_lo", "y")


def quantize_features(grad):
    rows, cols = grad.shape
    blocks = grad.reshape(rows // 32, 32, cols // 2, 2)
    scales = jnp.max(jnp.abs(blocks), axis=(1, 3)) + 1e-06
    mantissa = (blocks / scales[:, None, :, None]).reshape(grad.shape)
    return (mantissa.astype(jnp.bfloat16), scales)


def quantize_hidden(grad):
    rows, cols = grad.shape
    blocks = grad.reshape(rows // 2, 2, cols // 32, 32)
    scales = jnp.max(jnp.abs(blocks), axis=(1, 3)) + 1e-06
    mantissa = (blocks / scales[:, None, :, None]).reshape(grad.shape)
    return (mantissa.astype(jnp.bfloat16), scales)


def contract_last(left, right):
    return lax.dot_general(
        left, right, (((1,), (1,)), ((), ())), preferred_element_type=jnp.float32
    )


def contract_first(left, right):
    return lax.dot_general(
        left, right, (((0,), (0,)), ((), ())), preferred_element_type=jnp.float32
    )


def gate_terms(gate, up, hidden_grad):
    sigmoid_gate = jax.nn.sigmoid(gate)
    silu_gate = gate * sigmoid_gate
    hidden = (silu_gate * up).astype(jnp.bfloat16)
    gate_grad = (hidden_grad * up * sigmoid_gate * (1.0 + gate * (1.0 - sigmoid_gate))).astype(
        jnp.bfloat16
    )
    up_grad = (hidden_grad * silu_gate).astype(jnp.bfloat16)
    return (hidden, gate_grad, up_grad)


def pipe_exchange(parts):
    if PIPE_MODE == "flat_ar":
        gate, up, hidden_grad = lax.psum(tuple(parts), PIPE)
        return gate_terms(gate, up, hidden_grad)
    stacked = jnp.stack(parts)
    if PIPE_MODE == "flat":
        shard = lax.psum_scatter(stacked, PIPE, scatter_dimension=1, tiled=True)
    else:
        shard = stacked
        for axis in ("core", "x", "z_hi"):
            shard = lax.psum_scatter(shard, axis, scatter_dimension=1, tiled=True)
    products = jnp.stack(gate_terms(shard[0], shard[1], shard[2]))
    if PIPE_MODE == "flat":
        full = lax.all_gather(products, PIPE, axis=1, tiled=True)
    else:
        full = products
        for axis in ("z_hi", "x", "core"):
            full = lax.all_gather(full, axis, axis=1, tiled=True)
    return full[0], full[1], full[2]


def tensor_exchange(partial, n_zlo, n_y):
    if TENSOR_MODE == "flat":
        return lax.psum_scatter(partial, TENSOR, scatter_dimension=0, tiled=True)
    if TENSOR_MODE == "zlo_y":
        partial = lax.psum_scatter(partial, "z_lo", scatter_dimension=0, tiled=True)
        return lax.psum_scatter(partial, "y", scatter_dimension=0, tiled=True)
    rows, cols = partial.shape
    blocks = partial.reshape(n_zlo, n_y, rows // (n_zlo * n_y), cols)
    blocks = jnp.swapaxes(blocks, 0, 1).reshape(rows, cols)
    blocks = lax.psum_scatter(blocks, "y", scatter_dimension=0, tiled=True)
    return lax.psum_scatter(blocks, "z_lo", scatter_dimension=0, tiled=True)


def make_on_device(n_zlo, n_y):
    def on_device(tokens, out_grad, w_gate, w_up, w_down):
        gate_part = jnp.dot(tokens, w_gate, preferred_element_type=jnp.float32)
        up_part = jnp.dot(tokens, w_up, preferred_element_type=jnp.float32)
        hidden_part = contract_last(out_grad, w_down)
        hidden, gate_grad, up_grad = pipe_exchange((gate_part, up_part, hidden_part))
        input_grad = tensor_exchange(
            contract_last(gate_grad, w_gate) + contract_last(up_grad, w_up), n_zlo, n_y
        )
        gate_mantissa, gate_scales = quantize_features(contract_first(tokens, gate_grad))
        up_mantissa, up_scales = quantize_features(contract_first(tokens, up_grad))
        down_mantissa, down_scales = quantize_hidden(contract_first(hidden, out_grad))
        return (
            input_grad,
            gate_mantissa,
            gate_scales,
            up_mantissa,
            up_scales,
            down_mantissa,
            down_scales,
        )

    return on_device


def fine_mesh(mesh):
    n_pipe, n_tensor = mesh.shape["pipe"], mesh.shape["tensor"]
    n_y = 4
    n_zlo = n_tensor // n_y
    n_core = 2
    n_x = 4
    n_zhi = n_pipe // (n_core * n_x)
    devices = np.asarray(mesh.devices).reshape(n_zhi, n_x, n_core, n_zlo, n_y)
    return Mesh(devices, ("z_hi", "x", "core", "z_lo", "y")), n_zlo, n_y


def solution(mesh):
    fine, n_zlo, n_y = fine_mesh(mesh)
    in_specs = (
        P(None, PIPE),
        P(None, PIPE),
        P(PIPE, TENSOR),
        P(PIPE, TENSOR),
        P(TENSOR, PIPE),
    )
    out_specs = (
        P(TENSOR, PIPE),
        P(PIPE, TENSOR),
        P(PIPE, TENSOR),
        P(PIPE, TENSOR),
        P(PIPE, TENSOR),
        P(TENSOR, PIPE),
        P(TENSOR, PIPE),
    )
    return jax.shard_map(
        make_on_device(n_zlo, n_y),
        mesh=fine,
        in_specs=in_specs,
        out_specs=out_specs,
        check_vma=False,
    )
```

time: 569 us -> 277 us (0.49)
  waiting for transfers between devices: 404 us -> 175 us
  local copies, waits for them, and re-layouts: 129 us -> 32.7 us
  blocking collectives: 0 us -> 32.1 us
    psum x1 -> x0, waiting for transfers between devices: 293 us -> none  [on_device(): gate, up, hidden_grad = lax.psum((gate_part, up_part, hidden_part), 'pipe')]
    slice x6 -> x0, local copies, waits for them, and re-layouts: 120 us -> none  [the longest x4 80.6 us: quantize_features(): paired = jnp.maximum(mags[:, 0::2], mags[:, 1::2])]
    reduce_scatter x1 -> x5, waiting for transfers between devices: 111 us -> 162 us  [the longest x3 112 us: pipe_exchange(): shard = lax.psum_scatter(shard, axis, scatter_dimension=1, tiled=True)]
    all_gather x0 -> x2, blocking collectives: none -> 32.1 us  [pipe_exchange(): full = lax.all_gather(full, axis, axis=1, tiled=True)]
    all_gather x0 -> x1, waiting for transfers between devices: none -> 12.8 us  [pipe_exchange(): full = lax.all_gather(full, axis, axis=1, tiled=True)]
    div x6 -> x4, local copies, waits for them, and re-layouts: 4.02 us -> 14.1 us  [quantize_features(): mantissa = (blocks / scales[:, None, :, None]).reshape(grad.shape)]
    convert_element_type x0 -> x2, local copies, waits for them, and re-layouts: none -> 5.76 us  [quantize_hidden(): return (mantissa.astype(jnp.bfloat16), scales)]
  transfers between devices with their start and end apart: 2 -> 6, of which waited for: 2 -> 6; matrix products, arithmetic and copies ran while one was open for 24% -> 16% of each run, Pallas kernels for 0% -> 0%
where the time goes in v1:
time: 277 us; the launch traced here: 276 us
  waiting for transfers between devices  175 us (63%)
  local copies, waits for them, and re-layouts  32.7 us (12%)
  blocking collectives  32.1 us (12%)
  between operations  14.3 us (5%)
  other arithmetic  13.1 us (5%)
  matrix products  8.85 us (3%)
    reduce_scatter x3, waiting for transfers between devices, pipe_exchange(): shard = lax.psum_scatter(shard, axis, scatter_dimension=1, tiled=True)  112 us
    all_gather x2, blocking collectives, pipe_exchange(): full = lax.all_gather(full, axis, axis=1, tiled=True)  32.1 us
    reduce_scatter x1, waiting for transfers between devices, tensor_exchange(): partial = lax.psum_scatter(partial, 'z_lo', scatter_dimension=0, tiled=True)  30.7 us
    reduce_scatter x1, waiting for transfers between devices, tensor_exchange(): return lax.psum_scatter(partial, 'y', scatter_dimension=0, tiled=True)  19.5 us
    div x4, local copies, waits for them, and re-layouts, quantize_features(): mantissa = (blocks / scales[:, None, :, None]).reshape(grad.shape)  14.1 us
    all_gather x1, waiting for transfers between devices, pipe_exchange(): full = lax.all_gather(full, axis, axis=1, tiled=True)  12.8 us
    unnamed x25, local copies, waits for them, and re-layouts  7.51 us
    convert_element_type x2, local copies, waits for them, and re-layouts, quantize_hidden(): return (mantissa.astype(jnp.bfloat16), scales)  5.76 us
  transfers between devices with their start and end apart: 6, of which 6 were waited for; matrix products, arithmetic and copies ran while one was open for 16% of the time, Pallas kernels for 0%

profile of v1, /device:TPU:6, one launch (start us, length us, event | category | flops | bytes accessed | tf_op | source)
XLA Modules:
  0.0 276.1 jit_solution(17815208416039630571)
XLA Ops:
  7.3 1.0 copy-done
  8.2 1.5 convolution_bitcast_fusion.3
  10.6 1.9 pad_maximum_fusion
  12.6 26.1 %reduce-scatter.6.cloned.1.call-done = f32[3,256,512]{2,1,0:T(8,128)} async-done(((f32[3,512,512]{2,1,0:T(8,128)}), f32[3,256,512]{2,1,0:T(8,128)}) %reduce-scatter.6.cloned.1.call-update) | async-done | bytes 1572880 | tf_op jit(solution)/shard_map/reduce_scatter | solution.py:64
  38.8 36.7 %reduce-scatter.8.cloned.1.call-done = f32[3,64,512]{2,1,0:T(8,128)} async-done(((f32[3,256,512]{2,1,0:T(8,128)}), f32[3,64,512]{2,1,0:T(8,128)}) %reduce-scatter.8.cloned.1.call-update) | async-done | bytes 393232 | tf_op jit(solution)/shard_map/reduce_scatter | solution.py:64
  75.6 48.8 %reduce-scatter.10.cloned.1.call-done = f32[3,32,512]{2,1,0:T(8,128)} async-done(((f32[3,64,512]{2,1,0:T(8,128)}), f32[3,32,512]{2,1,0:T(8,128)}) %reduce-scatter.10.cloned.1.call-update) | async-done | bytes 196624 | tf_op jit(solution)/shard_map/reduce_scatter | solution.py:64
  124.3 0.9 multiply_convert_fusion.2
  125.3 17.1 %all_gather.9 = bf16[3,64,512]{2,1,0:T(8,128)(2,1)S(1)} all-gather(bf16[3,32,512]{2,1,0:T(8,128)(2,1)S(1)} %pad_maximum_fusion.1), channel_id=1, replica_groups=mesh['z_hi'=2,'x'=4,'core'=2,'z_lo'=8,'y'=4] {'z_hi'}, dimensions={1}, use_global_device_ids=true | all-gather | bytes 294912 | tf_op jit(solution)/shard_map/all_gather | solution.py:71
  142.4 15.0 %all_gather.10 = bf16[3,256,512]{2,1,0:T(8,128)(2,1)} all-gather(bf16[3,64,512]{2,1,0:T(8,128)(2,1)S(1)} %all_gather.9), channel_id=1, replica_groups=mesh['z_hi'=2,'x'=4,'core'=2,'z_lo'=8,'y'=4] {'x'}, dimensions={1}, use_global_device_ids=true | all-gather | bytes 983040 | tf_op jit(solution)/shard_map/all_gather | solution.py:71
  157.5 1.0 copy.27
  158.5 12.8 %all-gather.2.cloned.1.call-done = bf16[3,512,512]{2,1,0:T(8,128)(2,1)} async-done(((bf16[3,256,512]{2,1,0:T(8,128)(2,1)}), bf16[3,512,512]{2,1,0:T(8,128)(2,1)}) %all-gather.2.cloned.1.call-update) | async-done | bytes 1572880 | tf_op jit(solution)/shard_map/all_gather | solution.py:71
  171.3 1.6 fusion.2
  172.9 1.4 convolution_add_fusion
  174.6 1.5 fusion.4
  176.1 2.5 abs.16
  178.6 2.8 %reduce_max.27 = f32[16,256]{0,1:T(8,128)S(1)} reduce(f32[16,32,256,2]{1,0,3,2:T(8,128)} %abs.16, f32[]{:T(128)} %constant.0.clone.1), dimensions={1,3}, to_apply=%region_5.0 | reduce | flops 258048 | bytes 1064964 | tf_op jit(solution)/shard_map/reduce_max | solution.py:18
  182.1 2.5 div.37
  184.7 4.5 %div.38 = f32[512,512]{0,1:T(8,128)} reshape(f32[16,32,256,2]{1,0,3,2:T(8,128)} %div.37) | data formatting | bytes 2097152 | tf_op jit(solution)/shard_map/div | solution.py:19
  189.1 2.2 divide_convert_fusion.2
  191.4 2.1 copy.30
  193.4 1.5 fusion.5
  194.9 2.5 abs.18
  197.4 2.8 %reduce_max.28 = f32[16,256]{0,1:T(8,128)S(1)} reduce(f32[16,32,256,2]{1,0,3,2:T(8,128)} %abs.18, f32[]{:T(128)} %constant.0.clone.1), dimensions={1,3}, to_apply=%region_6.0 | reduce | flops 258048 | bytes 1064964 | tf_op jit(solution)/shard_map/reduce_max | solution.py:18
  200.2 0.7 copy.33
  200.9 2.5 div.40
  203.4 4.5 %div.41 = f32[512,512]{0,1:T(8,128)} reshape(f32[16,32,256,2]{1,0,3,2:T(8,128)} %div.40) | data formatting | bytes 2097152 | tf_op jit(solution)/shard_map/div | solution.py:19
  207.9 2.2 divide_convert_fusion.1
  210.1 2.1 copy.32
  213.2 30.7 %reduce-scatter.12.cloned.1.call-done = f32[64,512]{1,0:T(8,128)} async-done(((f32[512,512]{1,0:T(8,128)}), f32[64,512]{1,0:T(8,128)}) %reduce-scatter.12.cloned.1.call-update) | async-done | bytes 131088 | tf_op jit(solution)/shard_map/reduce_scatter | solution.py:79
  244.0 3.0 %copy.29 = bf16[256,2,16,32]{3,2,1,0:T(8,128)(2,1)S(1)} copy(bf16[256,2,16,32]{0,3,2,1:T(8,128)(2,1)S(1)} %divide_convert_fusion) | data formatting | bytes 1048576 | tf_op jit(solution)/shard_map/convert_element_type | solution.py:28
  247.1 2.8 convert_element_type.30
  249.8 19.5 %reduce-scatter.14.cloned.1.call-done = f32[16,512]{1,0:T(8,128)} async-done(((f32[64,512]{1,0:T(8,128)}), f32[16,512]{1,0:T(8,128)}) %reduce-scatter.14.cloned.1.call-update) | async-done | bytes 32784 | tf_op jit(solution)/shard_map/reduce_scatter | solution.py:80
  (43 shorter events, 3.2 us)
Async XLA Ops:
  7.2 1.0 copy-start
  7.2 2.5 copy-start.5
  7.2 2.9 %copy-start.4 = (bf16[512,512]{1,0:T(8,128)(2,1)S(1)}, bf16[512,512]{1,0:T(8,128)(2,1)}, u32[]{:S(2)}) copy-start(bf16[512,512]{1,0:T(8,128)(2,1)} %param.6) | copy-start | bytes 1572868
  7.2 2.9 %copy-start.8 = (bf16[512,512]{1,0:T(8,128)(2,1)S(1)}, bf16[512,512]{1,0:T(8,128)(2,1)}, u32[]{:S(2)}) copy-start(bf16[512,512]{1,0:T(8,128)(2,1)} %param.9) | copy-start | bytes 1572868
  7.2 31.5 %reduce-scatter.6.cloned.1.call-start = ((), (), s32[]{:S(2)}) async-start(), calls=%async_computation.5 | async-start | bytes 4718592 | tf_op jit(solution)/shard_map/reduce_scatter | solution.py:64
  12.6 62.9 %reduce-scatter.8.cloned.1.call-start = ((), (), s32[]{:S(2)}) async-start(), calls=%async_computation.6 | async-start | bytes 1966080 | tf_op jit(solution)/shard_map/reduce_scatter | solution.py:64
  38.8 85.5 %reduce-scatter.10.cloned.1.call-start = ((), (), s32[]{:S(2)}) async-start(), calls=%async_computation.7 | async-start | bytes 589824 | tf_op jit(solution)/shard_map/reduce_scatter | solution.py:64
  75.5 95.8 %all-gather.2.cloned.1.call-start = ((), (), s32[]{:S(2)}) async-start(), calls=%async_computation.8 | async-start | bytes 2359296 | tf_op jit(solution)/shard_map/all_gather | solution.py:71
  157.4 15.5 %copy-start.6 = (bf16[512,512]{1,0:T(8,128)(2,1)S(1)}, bf16[512,512]{1,0:T(8,128)(2,1)}, u32[]{:S(2)}) copy-start(bf16[512,512]{1,0:T(8,128)(2,1)} %param.8) | copy-start | bytes 1572868
  157.4 86.5 %reduce-scatter.12.cloned.1.call-start = ((), (), s32[]{:S(2)}) async-start(), calls=%async_computation.9 | async-start | bytes 1179648 | tf_op jit(solution)/shard_map/reduce_scatter | solution.py:79
  171.3 1.6 copy-start.1
  174.4 94.9 %reduce-scatter.14.cloned.1.call-start = ((), (), s32[]{:S(2)}) async-start(), calls=%async_computation.10 | async-start | bytes 163840 | tf_op jit(solution)/shard_map/reduce_scatter | solution.py:80
  184.7 4.5 %copy-start.3 = (f32[512,512]{0,1:T(8,128)S(1)}, f32[512,512]{0,1:T(8,128)}, u32[]{:S(2)}) copy-start(f32[512,512]{0,1:T(8,128)} %get-tuple-element.32) | copy-start | bytes 3145732
  203.4 4.5 %copy-start.2 = (f32[512,512]{0,1:T(8,128)S(1)}, f32[512,512]{0,1:T(8,128)}, u32[]{:S(2)}) copy-start(f32[512,512]{0,1:T(8,128)} %get-tuple-element.34) | copy-start | bytes 3145732
  210.1 2.6 copy-start.7
  213.2 33.8 %copy-start.9 = (f32[256,16]{0,1:T(8,128)}, f32[256,16]{0,1:T(8,128)S(1)}, u32[]{:S(2)}) copy-start(f32[256,16]{0,1:T(8,128)S(1)} %broadcast_add_fusion.2) | copy-start | bytes 49156
Sparse Core Ops, SparseCore 0:
  12.7 25.9 reduce-scatter.5
  41.6 33.8 reduce-scatter.7
  78.3 45.9 reduce-scatter.9
  157.5 13.7 all-gather.1
  174.5 69.3 reduce-scatter.11
  247.1 22.1 reduce-scatter.13

commit v2 on v1

v2 whole, which is shorter than its diff:
```python
import jax
import jax.numpy as jnp
import numpy as np
from jax import lax
from jax.sharding import Mesh
from jax.sharding import PartitionSpec as P

PIPE_MODE = "ppermute"
TENSOR_MODE = "ppermute"

FINE = ("z_hi", "x2", "x1", "core", "z4", "z2", "z1", "y2", "y1")
PIPE = ("z_hi", "x2", "x1", "core")
TENSOR = ("z4", "z2", "z1", "y2", "y1")
PIPE_STAGES = ("core", "x1", "x2", "z_hi")
TENSOR_STAGES = ("z1", "z2", "z4", "y1", "y2")


def quantize_features(grad):
    rows, cols = grad.shape
    blocks = grad.reshape(rows // 32, 32, cols // 2, 2)
    scales = jnp.max(jnp.abs(blocks), axis=(1, 3)) + 1e-06
    mantissa = (blocks / scales[:, None, :, None]).reshape(grad.shape)
    return (mantissa.astype(jnp.bfloat16), scales)


def quantize_hidden(grad):
    rows, cols = grad.shape
    blocks = grad.reshape(rows // 2, 2, cols // 32, 32)
    scales = jnp.max(jnp.abs(blocks), axis=(1, 3)) + 1e-06
    mantissa = (blocks / scales[:, None, :, None]).reshape(grad.shape)
    return (mantissa.astype(jnp.bfloat16), scales)


def contract_last(left, right):
    return lax.dot_general(
        left, right, (((1,), (1,)), ((), ())), preferred_element_type=jnp.float32
    )


def contract_first(left, right):
    return lax.dot_general(
        left, right, (((0,), (0,)), ((), ())), preferred_element_type=jnp.float32
    )


def gate_terms(gate, up, hidden_grad):
    sigmoid_gate = jax.nn.sigmoid(gate)
    silu_gate = gate * sigmoid_gate
    hidden = (silu_gate * up).astype(jnp.bfloat16)
    gate_grad = (hidden_grad * up * sigmoid_gate * (1.0 + gate * (1.0 - sigmoid_gate))).astype(
        jnp.bfloat16
    )
    up_grad = (hidden_grad * silu_gate).astype(jnp.bfloat16)
    return (hidden, gate_grad, up_grad)


def halve(x, axis, dim, mode):
    if mode == "xla":
        return lax.psum_scatter(x, axis, scatter_dimension=dim, tiled=True)
    half = x.shape[dim] // 2
    me = lax.axis_index(axis)
    keep = lax.dynamic_slice_in_dim(x, me * half, half, axis=dim)
    send = lax.dynamic_slice_in_dim(x, (1 - me) * half, half, axis=dim)
    return keep + lax.ppermute(send, axis, perm=[(0, 1), (1, 0)])


def double(x, axis, dim, mode):
    if mode == "xla":
        return lax.all_gather(x, axis, axis=dim, tiled=True)
    me = lax.axis_index(axis)
    other = lax.ppermute(x, axis, perm=[(0, 1), (1, 0)])
    both = jnp.concatenate([other, other], axis=dim)
    return lax.dynamic_update_slice_in_dim(both, x, me * x.shape[dim], axis=dim)


def pipe_exchange(parts):
    shard = jnp.stack(parts)
    for axis in PIPE_STAGES:
        shard = halve(shard, axis, 1, PIPE_MODE)
    full = jnp.stack(gate_terms(shard[0], shard[1], shard[2]))
    for axis in reversed(PIPE_STAGES):
        full = double(full, axis, 1, PIPE_MODE)
    return full[0], full[1], full[2]


def tensor_exchange(partial):
    rows, cols = partial.shape
    bits = len(TENSOR)
    blocks = partial.reshape((2,) * bits + (rows >> bits, cols))
    order = [TENSOR.index(a) for a in TENSOR_STAGES]
    blocks = jnp.transpose(blocks, order + [bits, bits + 1]).reshape(rows, cols)
    for axis in TENSOR_STAGES:
        blocks = halve(blocks, axis, 0, TENSOR_MODE)
    return blocks


def make_on_device():
    def on_device(tokens, out_grad, w_gate, w_up, w_down):
        gate_part = jnp.dot(tokens, w_gate, preferred_element_type=jnp.float32)
        up_part = jnp.dot(tokens, w_up, preferred_element_type=jnp.float32)
        hidden_part = contract_last(out_grad, w_down)
        hidden, gate_grad, up_grad = pipe_exchange((gate_part, up_part, hidden_part))
        input_grad = tensor_exchange(
            contract_last(gate_grad, w_gate) + contract_last(up_grad, w_up)
        )
        gate_mantissa, gate_scales = quantize_features(contract_first(tokens, gate_grad))
        up_mantissa, up_scales = quantize_features(contract_first(tokens, up_grad))
        down_mantissa, down_scales = quantize_hidden(contract_first(hidden, out_grad))
        return (
            input_grad,
            gate_mantissa,
            gate_scales,
            up_mantissa,
            up_scales,
            down_mantissa,
            down_scales,
        )

    return on_device


def fine_mesh(mesh):
    n_pipe, n_tensor = mesh.shape["pipe"], mesh.shape["tensor"]
    assert n_pipe == 16 and n_tensor == 32
    devices = np.asarray(mesh.devices).reshape((2,) * len(FINE))
    return Mesh(devices, FINE)


def solution(mesh):
    fine = fine_mesh(mesh)
    in_specs = (
        P(None, PIPE),
        P(None, PIPE),
        P(PIPE, TENSOR),
        P(PIPE, TENSOR),
        P(TENSOR, PIPE),
    )
    out_specs = (
        P(TENSOR, PIPE),
        P(PIPE, TENSOR),
        P(PIPE, TENSOR),
        P(PIPE, TENSOR),
        P(PIPE, TENSOR),
        P(TENSOR, PIPE),
        P(TENSOR, PIPE),
    )
    return jax.shard_map(
        make_on_device(),
        mesh=fine,
        in_specs=in_specs,
        out_specs=out_specs,
        check_vma=False,
    )
```

time: 277 us -> 226 us (0.82)
  waiting for transfers between devices: 175 us -> 94.7 us
  starting transfers between devices: 0.42 us -> 65.3 us
  blocking collectives: 32.1 us -> 0 us
  between operations: 14.3 us -> 1.21 us
  local copies, waits for them, and re-layouts: 32.7 us -> 39.8 us
    reduce_scatter x5 -> x0, waiting for transfers between devices: 162 us -> none  [the longest x3 112 us: pipe_exchange(): shard = lax.psum_scatter(shard, axis, scatter_dimension=1, tiled=True)]
    ppermute x0 -> x13, waiting for transfers between devices: none -> 94.7 us  [the longest x9 73.9 us: halve(): return keep + lax.ppermute(send, axis, perm=[(0, 1), (1, 0)])]
    ppermute x0 -> x13, starting transfers between devices: none -> 65.3 us  [the longest x9 45.6 us: halve(): return keep + lax.ppermute(send, axis, perm=[(0, 1), (1, 0)])]
    all_gather x2 -> x0, blocking collectives: 32.1 us -> none  [pipe_exchange(): full = lax.all_gather(full, axis, axis=1, tiled=True)]
    all_gather x1 -> x0, waiting for transfers between devices: 12.8 us -> none  [pipe_exchange(): full = lax.all_gather(full, axis, axis=1, tiled=True)]
    add x0 -> x9, other arithmetic: none -> 5.39 us  [halve(): return keep + lax.ppermute(send, axis, perm=[(0, 1), (1, 0)])]
    convert_element_type x2, other arithmetic: 4.43 us -> 0.5 us  [quantize_features(): return (mantissa.astype(jnp.bfloat16), scales)]
    unnamed x25 -> x35, local copies, waits for them, and re-layouts: 7.51 us -> 9.44 us
  transfers between devices with their start and end apart: 6 -> 13, of which waited for: 6 -> 11; matrix products, arithmetic and copies ran while one was open for 16% -> 18% of each run, Pallas kernels for 0% -> 0%
where the time goes in v2:
time: 226 us; the launch traced here: 225 us
  waiting for transfers between devices  94.7 us (42%)
  starting transfers between devices  65.3 us (29%)
  local copies, waits for them, and re-layouts  39.8 us (18%)
  other arithmetic  14.8 us (7%)
  matrix products  9.11 us (4%)
    ppermute x9, waiting for transfers between devices, halve(): return keep + lax.ppermute(send, axis, perm=[(0, 1), (1, 0)])  73.9 us
    ppermute x9, starting transfers between devices, halve(): return keep + lax.ppermute(send, axis, perm=[(0, 1), (1, 0)])  45.6 us
    ppermute x4, waiting for transfers between devices, double(): other = lax.ppermute(x, axis, perm=[(0, 1), (1, 0)])  20.8 us
    ppermute x4, starting transfers between devices, double(): other = lax.ppermute(x, axis, perm=[(0, 1), (1, 0)])  19.8 us
    div x4, local copies, waits for them, and re-layouts, quantize_features(): mantissa = (blocks / scales[:, None, :, None]).reshape(grad.shape)  13.8 us
    unnamed x35, local copies, waits for them, and re-layouts  9.44 us
    abs x2, local copies, waits for them, and re-layouts, quantize_features(): scales = jnp.max(jnp.abs(blocks), axis=(1, 3)) + 1e-06  6.29 us
    convert_element_type x2, local copies, waits for them, and re-layouts, quantize_hidden(): return (mantissa.astype(jnp.bfloat16), scales)  5.75 us
  transfers between devices with their start and end apart: 13, of which 11 were waited for; matrix products, arithmetic and copies ran while one was open for 18% of the time, Pallas kernels for 0%

profile of v2, /device:TPU:6, one launch (start us, length us, event | category | flops | bytes accessed | tf_op | source)
XLA Modules:
  0.0 225.0 jit_solution(4163117636727164919)
XLA Ops:
  4.2 2.5 %convolution_bitcast_fusion.2 = f32[1,512,512]{2,1,0:T(8,128)} fusion(bf16[512,512]{1,0:T(8,128)(2,1)S(1)} %copy-done.8, bf16[512,512]{1,0:T(8,128)(2,1)} %param.9), kind=kOutput, calls=%fused_computation.6 | convolution fusion | flops 268435456 | bytes 2097152 | tf_op jit(solution)/shard_map/dot_general | solution.py:35
  11.8 3.5 %collective-permute-done = f32[3,256,512]{2,1,0:T(8,128)} collective-permute-done((f32[3,256,512]{2,1,0:T(8,128)S(1)}, f32[3,256,512]{2,1,0:T(8,128)}, u32[]{:S(2)}, u32[]{:S(2)}) %collective-permute-start) | collective-permute-done | bytes 1572896 | tf_op jit(solution)/shard_map/ppermute | solution.py:64
  15.3 2.2 dynamic-slice_add_fusion
  17.6 2.7 %collective-permute-start.1 = (f32[3,128,512]{2,1,0:T(8,128)S(1)}, f32[3,128,512]{2,1,0:T(8,128)}, u32[]{:S(2)}, u32[]{:S(2)}) collective-permute-start(f32[3,128,512]{2,1,0:T(8,128)S(1)} %constant_dynamic-slice_fusion.7), channel_id=1, source_target_pairs={{0,64},{64,0},{1,65},{65,1},{2,66},{66,2},{3,67},{67,3},{4,68},{68... | collective-permute-start | bytes 2359304 | tf_op jit(solution)/shard_map/ppermute | solution.py:64
  20.4 18.8 %collective-permute-done.1 = f32[3,128,512]{2,1,0:T(8,128)} collective-permute-done((f32[3,128,512]{2,1,0:T(8,128)S(1)}, f32[3,128,512]{2,1,0:T(8,128)}, u32[]{:S(2)}, u32[]{:S(2)}) %collective-permute-start.1) | collective-permute-done | bytes 786464 | tf_op jit(solution)/shard_map/ppermute | solution.py:64
  40.5 7.5 %collective-permute-start.2 = (f32[3,64,512]{2,1,0:T(8,128)S(1)}, f32[3,64,512]{2,1,0:T(8,128)S(1)}, u32[]{:S(2)}, u32[]{:S(2)}) collective-permute-start(f32[3,64,512]{2,1,0:T(8,128)S(1)} %constant_dynamic-slice_fusion.6), channel_id=1, source_target_pairs={{0,128},{128,0},{1,129},{129,1},{2,130},{130,2},{3,131},{131,3},{4... | collective-permute-start | bytes 1179656 | tf_op jit(solution)/shard_map/ppermute | solution.py:64
  48.0 8.8 %collective-permute-done.2 = f32[3,64,512]{2,1,0:T(8,128)S(1)} collective-permute-done((f32[3,64,512]{2,1,0:T(8,128)S(1)}, f32[3,64,512]{2,1,0:T(8,128)S(1)}, u32[]{:S(2)}, u32[]{:S(2)}) %collective-permute-start.2) | collective-permute-done | bytes 393248 | tf_op jit(solution)/shard_map/ppermute | solution.py:64
  56.9 13.1 %collective-permute-start.3 = (f32[3,32,512]{2,1,0:T(8,128)S(1)}, f32[3,32,512]{2,1,0:T(8,128)S(1)}, u32[]{:S(2)}, u32[]{:S(2)}) collective-permute-start(f32[3,32,512]{2,1,0:T(8,128)S(1)} %constant_dynamic-slice_fusion.5), channel_id=1, source_target_pairs={{0,256},{256,0},{1,257},{257,1},{2,258},{258,2},{3,259},{259,3},{4... | collective-permute-start | bytes 589832 | tf_op jit(solution)/shard_map/ppermute | solution.py:64
  70.0 13.9 %collective-permute-done.3 = f32[3,32,512]{2,1,0:T(8,128)S(1)} collective-permute-done((f32[3,32,512]{2,1,0:T(8,128)S(1)}, f32[3,32,512]{2,1,0:T(8,128)S(1)}, u32[]{:S(2)}, u32[]{:S(2)}) %collective-permute-start.3) | collective-permute-done | bytes 196640 | tf_op jit(solution)/shard_map/ppermute | solution.py:64
  84.1 13.2 %collective-permute-start.4 = (bf16[3,32,512]{2,1,0:T(8,128)(2,1)S(1)}, bf16[3,32,512]{2,1,0:T(8,128)(2,1)S(1)}, u32[]{:S(2)}, u32[]{:S(2)}) collective-permute-start(bf16[3,32,512]{2,1,0:T(8,128)(2,1)S(1)} %pad_maximum_fusion.5), channel_id=1, source_target_pairs={{0,256},{256,0},{1,257},{257,1},{2,258},{258,2},{3,259},{259,3},{4... | collective-permute-start | bytes 294920 | tf_op jit(solution)/shard_map/ppermute | solution.py:71
  97.3 3.3 %collective-permute-done.4 = bf16[3,32,512]{2,1,0:T(8,128)(2,1)S(1)} collective-permute-done((bf16[3,32,512]{2,1,0:T(8,128)(2,1)S(1)}, bf16[3,32,512]{2,1,0:T(8,128)(2,1)S(1)}, u32[]{:S(2)}, u32[]{:S(2)}) %collective-permute-start.4) | collective-permute-done | bytes 98336 | tf_op jit(solution)/shard_map/ppermute | solution.py:71
  102.5 9.2 %collective-permute-done.5 = bf16[3,64,512]{2,1,0:T(8,128)(2,1)S(1)} collective-permute-done((bf16[3,64,512]{2,1,0:T(8,128)(2,1)S(1)}, bf16[3,64,512]{2,1,0:T(8,128)(2,1)S(1)}, u32[]{:S(2)}, u32[]{:S(2)}) %collective-permute-start.5) | collective-permute-done | bytes 196640 | tf_op jit(solution)/shard_map/ppermute | solution.py:71
  111.8 2.7 %collective-permute-start.6 = (bf16[3,128,512]{2,1,0:T(8,128)(2,1)S(1)}, bf16[3,128,512]{2,1,0:T(8,128)(2,1)S(1)}, u32[]{:S(2)}, u32[]{:S(2)}) collective-permute-start(bf16[3,128,512]{2,1,0:T(8,128)(2,1)S(1)} %constant_dynamic-update-slice_fusion.2), channel_id=1, source_target_pairs={{0,64},{64,0},{1,65},{65,1},{2,66},{66,2},{3,67},{67,3},{4,68},{68... | collective-permute-start | bytes 1179656 | tf_op jit(solution)/shard_map/ppermute | solution.py:71
  114.6 6.9 %collective-permute-done.6 = bf16[3,128,512]{2,1,0:T(8,128)(2,1)S(1)} collective-permute-done((bf16[3,128,512]{2,1,0:T(8,128)(2,1)S(1)}, bf16[3,128,512]{2,1,0:T(8,128)(2,1)S(1)}, u32[]{:S(2)}, u32[]{:S(2)}) %collective-permute-start.6) | collective-permute-done | bytes 393248 | tf_op jit(solution)/shard_map/ppermute | solution.py:71
  121.6 1.9 collective-permute-start.7
  133.6 6.4 %collective-permute-start.8 = (f32[256,512]{1,0:T(8,128)}, f32[256,512]{1,0:T(8,128)}, u32[]{:S(2)}, u32[]{:S(2)}) collective-permute-start(f32[256,512]{1,0:T(8,128)} %constant_dynamic-slice_fusion.4), channel_id=1, source_target_pairs={{0,4},{4,0},{1,5},{5,1},{2,6},{6,2},{3,7},{7,3},{8,12},{12,8},{9,1... | collective-permute-start | bytes 1572872 | tf_op jit(solution)/shard_map/ppermute | solution.py:64
  140.0 3.8 %abs.16 = f32[16,32,256,2]{1,0,3,2:T(8,128)} reshape(f32[512,512]{0,1:T(8,128)} %get-tuple-element.31) | data formatting | bytes 2097152 | tf_op jit(solution)/shard_map/abs | solution.py:21
  143.8 2.8 %reduce_max.27 = f32[16,256]{0,1:T(8,128)S(1)} reduce(f32[16,32,256,2]{1,0,3,2:T(8,128)} %abs.16, f32[]{:T(128)} %constant.55.clone.1), dimensions={1,3}, to_apply=%region_0.0 | reduce | flops 258048 | bytes 1064964 | tf_op jit(solution)/shard_map/reduce_max | solution.py:21
  146.7 2.5 %div.37 = f32[16,32,256,2]{1,0,3,2:T(8,128)} broadcast(f32[16,256]{0,1:T(8,128)S(1)} %broadcast_add_fusion.1), dimensions={0,2} | broadcast | bytes 1064960 | tf_op jit(solution)/shard_map/div | solution.py:22
  149.2 4.4 %div.38 = f32[512,512]{0,1:T(8,128)} reshape(f32[16,32,256,2]{1,0,3,2:T(8,128)} %div.37) | data formatting | bytes 2097152 | tf_op jit(solution)/shard_map/div | solution.py:22
  153.6 2.5 %abs.18 = f32[16,32,256,2]{1,0,3,2:T(8,128)} reshape(f32[512,512]{0,1:T(8,128)S(1)} %get-tuple-element.33) | data formatting | bytes 2097152 | tf_op jit(solution)/shard_map/abs | solution.py:21
  156.1 2.8 %reduce_max.28 = f32[16,256]{0,1:T(8,128)S(1)} reduce(f32[16,32,256,2]{1,0,3,2:T(8,128)} %abs.18, f32[]{:T(128)} %constant.55.clone.1), dimensions={1,3}, to_apply=%region_1.0 | reduce | flops 258048 | bytes 1064964 | tf_op jit(solution)/shard_map/reduce_max | solution.py:21
  158.9 2.5 %div.40 = f32[16,32,256,2]{1,0,3,2:T(8,128)} broadcast(f32[16,256]{0,1:T(8,128)S(1)} %broadcast_add_fusion), dimensions={0,2} | broadcast | bytes 1064960 | tf_op jit(solution)/shard_map/div | solution.py:22
  161.5 4.4 %div.41 = f32[512,512]{0,1:T(8,128)} reshape(f32[16,32,256,2]{1,0,3,2:T(8,128)} %div.40) | data formatting | bytes 2097152 | tf_op jit(solution)/shard_map/div | solution.py:22
  173.6 14.0 %collective-permute-done.9 = f32[128,512]{1,0:T(8,128)S(1)} collective-permute-done((f32[128,512]{1,0:T(8,128)S(1)}, f32[128,512]{1,0:T(8,128)S(1)}, u32[]{:S(2)}, u32[]{:S(2)}) %collective-permute-start.9) | collective-permute-done | bytes 262176 | tf_op jit(solution)/shard_map/ppermute | solution.py:64
  187.7 3.4 %collective-permute-start.10 = (f32[64,512]{1,0:T(8,128)S(1)}, f32[64,512]{1,0:T(8,128)S(1)}, u32[]{:S(2)}, u32[]{:S(2)}) collective-permute-start(f32[64,512]{1,0:T(8,128)S(1)} %constant_dynamic-slice_fusion.2), channel_id=1, source_target_pairs={{0,16},{16,0},{1,17},{17,1},{2,18},{18,2},{3,19},{19,3},{4,20},{20... | collective-permute-start | bytes 393224 | tf_op jit(solution)/shard_map/ppermute | solution.py:64
  191.6 12.2 %collective-permute-done.10 = f32[64,512]{1,0:T(8,128)S(1)} collective-permute-done((f32[64,512]{1,0:T(8,128)S(1)}, f32[64,512]{1,0:T(8,128)S(1)}, u32[]{:S(2)}, u32[]{:S(2)}) %collective-permute-start.10) | collective-permute-done | bytes 131104 | tf_op jit(solution)/shard_map/ppermute | solution.py:64
  203.8 3.5 %collective-permute-start.11 = (f32[32,512]{1,0:T(8,128)S(1)}, f32[32,512]{1,0:T(8,128)S(1)}, u32[]{:S(2)}, u32[]{:S(2)}) collective-permute-start(f32[32,512]{1,0:T(8,128)S(1)} %constant_dynamic-slice_fusion.1), channel_id=1, source_target_pairs={{0,1},{1,0},{2,3},{3,2},{4,5},{5,4},{6,7},{7,6},{8,9},{9,8},{10,11... | collective-permute-start | bytes 196616 | tf_op jit(solution)/shard_map/ppermute | solution.py:64
  207.3 2.6 %collective-permute-done.11 = f32[32,512]{1,0:T(8,128)S(1)} collective-permute-done((f32[32,512]{1,0:T(8,128)S(1)}, f32[32,512]{1,0:T(8,128)S(1)}, u32[]{:S(2)}, u32[]{:S(2)}) %collective-permute-start.11) | collective-permute-done | bytes 65568 | tf_op jit(solution)/shard_map/ppermute | solution.py:64
  210.0 5.1 %collective-permute-start.12 = (f32[16,512]{1,0:T(8,128)S(1)}, f32[16,512]{1,0:T(8,128)S(1)}, u32[]{:S(2)}, u32[]{:S(2)}) collective-permute-start(f32[16,512]{1,0:T(8,128)S(1)} %constant_dynamic-slice_fusion), channel_id=1, source_target_pairs={{0,2},{2,0},{1,3},{3,1},{4,6},{6,4},{5,7},{7,5},{8,10},{10,8},{9,1... | collective-permute-start | bytes 98312 | tf_op jit(solution)/shard_map/ppermute | solution.py:64
  218.6 3.0 %copy.32 = bf16[256,2,16,32]{3,2,1,0:T(8,128)(2,1)S(1)} copy(bf16[256,2,16,32]{0,3,2,1:T(8,128)(2,1)S(1)} %divide_convert_fusion) | data formatting | bytes 1048576 | tf_op jit(solution)/shard_map/convert_element_type | solution.py:31
  221.6 2.8 %convert_element_type.30 = bf16[512,512]{1,0:T(8,128)(2,1)} reshape(bf16[256,2,16,32]{3,2,1,0:T(8,128)(2,1)S(1)} %copy.32) | data formatting | bytes 1048576 | tf_op jit(solution)/shard_map/convert_element_type | solution.py:31
  (86 shorter events, 34.7 us)
Async XLA Ops:
  0.6 1.0 copy-start
  0.6 2.5 %copy-start.10 = (bf16[512,512]{1,0:T(8,128)(2,1)S(1)}, bf16[512,512]{1,0:T(8,128)(2,1)}, u32[]{:S(2)}) copy-start(bf16[512,512]{1,0:T(8,128)(2,1)} %param.7) | copy-start | bytes 1572868
  3.2 1.0 copy-start.8
  8.2 1.6 copy-start.1
  9.9 5.4 %collective-permute-start = (f32[3,256,512]{2,1,0:T(8,128)S(1)}, f32[3,256,512]{2,1,0:T(8,128)}, u32[]{:S(2)}, u32[]{:S(2)}) collective-permute-start(f32[3,256,512]{2,1,0:T(8,128)S(1)} %constant_dynamic-slice_fusion.8), channel_id=1, source_target_pairs={{0,32},{32,0},{1,33},{33,1},{2,34},{34,2},{3,35},{35,3},{4,36},{36... | collective-permute-start | bytes 4718600 | tf_op jit(solution)/shard_map/ppermute | solution.py:64
  17.6 21.6 %collective-permute-start.1 = (f32[3,128,512]{2,1,0:T(8,128)S(1)}, f32[3,128,512]{2,1,0:T(8,128)}, u32[]{:S(2)}, u32[]{:S(2)}) collective-permute-start(f32[3,128,512]{2,1,0:T(8,128)S(1)} %constant_dynamic-slice_fusion.7), channel_id=1, source_target_pairs={{0,64},{64,0},{1,65},{65,1},{2,66},{66,2},{3,67},{67,3},{4,68},{68... | collective-permute-start | bytes 2359304 | tf_op jit(solution)/shard_map/ppermute | solution.py:64
  40.5 16.3 %collective-permute-start.2 = (f32[3,64,512]{2,1,0:T(8,128)S(1)}, f32[3,64,512]{2,1,0:T(8,128)S(1)}, u32[]{:S(2)}, u32[]{:S(2)}) collective-permute-start(f32[3,64,512]{2,1,0:T(8,128)S(1)} %constant_dynamic-slice_fusion.6), channel_id=1, source_target_pairs={{0,128},{128,0},{1,129},{129,1},{2,130},{130,2},{3,131},{131,3},{4... | collective-permute-start | bytes 1179656 | tf_op jit(solution)/shard_map/ppermute | solution.py:64
  56.9 27.1 %collective-permute-start.3 = (f32[3,32,512]{2,1,0:T(8,128)S(1)}, f32[3,32,512]{2,1,0:T(8,128)S(1)}, u32[]{:S(2)}, u32[]{:S(2)}) collective-permute-start(f32[3,32,512]{2,1,0:T(8,128)S(1)} %constant_dynamic-slice_fusion.5), channel_id=1, source_target_pairs={{0,256},{256,0},{1,257},{257,1},{2,258},{258,2},{3,259},{259,3},{4... | collective-permute-start | bytes 589832 | tf_op jit(solution)/shard_map/ppermute | solution.py:64
  84.1 16.5 %collective-permute-start.4 = (bf16[3,32,512]{2,1,0:T(8,128)(2,1)S(1)}, bf16[3,32,512]{2,1,0:T(8,128)(2,1)S(1)}, u32[]{:S(2)}, u32[]{:S(2)}) collective-permute-start(bf16[3,32,512]{2,1,0:T(8,128)(2,1)S(1)} %pad_maximum_fusion.5), channel_id=1, source_target_pairs={{0,256},{256,0},{1,257},{257,1},{2,258},{258,2},{3,259},{259,3},{4... | collective-permute-start | bytes 294920 | tf_op jit(solution)/shard_map/ppermute | solution.py:71
  100.6 11.2 %collective-permute-start.5 = (bf16[3,64,512]{2,1,0:T(8,128)(2,1)S(1)}, bf16[3,64,512]{2,1,0:T(8,128)(2,1)S(1)}, u32[]{:S(2)}, u32[]{:S(2)}) collective-permute-start(bf16[3,64,512]{2,1,0:T(8,128)(2,1)S(1)} %constant_dynamic-update-slice_fusion.3), channel_id=1, source_target_pairs={{0,128},{128,0},{1,129},{129,1},{2,130},{130,2},{3,131},{131,3},{4... | collective-permute-start | bytes 589832 | tf_op jit(solution)/shard_map/ppermute | solution.py:71
  111.8 9.7 %collective-permute-start.6 = (bf16[3,128,512]{2,1,0:T(8,128)(2,1)S(1)}, bf16[3,128,512]{2,1,0:T(8,128)(2,1)S(1)}, u32[]{:S(2)}, u32[]{:S(2)}) collective-permute-start(bf16[3,128,512]{2,1,0:T(8,128)(2,1)S(1)} %constant_dynamic-update-slice_fusion.2), channel_id=1, source_target_pairs={{0,64},{64,0},{1,65},{65,1},{2,66},{66,2},{3,67},{67,3},{4,68},{68... | collective-permute-start | bytes 1179656 | tf_op jit(solution)/shard_map/ppermute | solution.py:71
  121.6 4.3 %collective-permute-start.7 = (bf16[3,256,512]{2,1,0:T(8,128)(2,1)S(1)}, bf16[3,256,512]{2,1,0:T(8,128)(2,1)}, u32[]{:S(2)}, u32[]{:S(2)}) collective-permute-start(bf16[3,256,512]{2,1,0:T(8,128)(2,1)S(1)} %constant_dynamic-update-slice_fusion.1), channel_id=1, source_target_pairs={{0,32},{32,0},{1,33},{33,1},{2,34},{34,2},{3,35},{35,3},{4,36},{36... | collective-permute-start | bytes 2359304 | tf_op jit(solution)/shard_map/ppermute | solution.py:71
  124.6 2.9 %copy-start.9 = (bf16[512,512]{1,0:T(8,128)(2,1)S(1)}, bf16[512,512]{1,0:T(8,128)(2,1)}, u32[]{:S(2)}) copy-start(bf16[512,512]{1,0:T(8,128)(2,1)} %param.8) | copy-start | bytes 1572868
  129.8 1.4 copy-start.11
  131.8 1.0 copy-start.6
  133.6 35.7 %collective-permute-start.8 = (f32[256,512]{1,0:T(8,128)}, f32[256,512]{1,0:T(8,128)}, u32[]{:S(2)}, u32[]{:S(2)}) collective-permute-start(f32[256,512]{1,0:T(8,128)} %constant_dynamic-slice_fusion.4), channel_id=1, source_target_pairs={{0,4},{4,0},{1,5},{5,1},{2,6},{6,2},{3,7},{7,3},{8,12},{12,8},{9,1... | collective-permute-start | bytes 1572872 | tf_op jit(solution)/shard_map/ppermute | solution.py:64
  165.8 3.2 %copy-start.3 = (f32[512,512]{0,1:T(8,128)S(1)}, f32[512,512]{0,1:T(8,128)}, u32[]{:S(2)}) copy-start(f32[512,512]{0,1:T(8,128)} %get-tuple-element.32) | copy-start | bytes 3145732
  166.7 2.3 %copy-start.5 = (f32[512,512]{0,1:T(8,128)S(1)}, f32[512,512]{0,1:T(8,128)}, u32[]{:S(2)}) copy-start(f32[512,512]{0,1:T(8,128)} %div.38) | copy-start | bytes 3145732
  169.0 1.2 copy-start.7
  169.3 4.1 %copy-start.2 = (f32[512,512]{0,1:T(8,128)S(1)}, f32[512,512]{0,1:T(8,128)}, u32[]{:S(2)}) copy-start(f32[512,512]{0,1:T(8,128)} %get-tuple-element.34) | copy-start | bytes 3145732
  169.3 4.1 %copy-start.4 = (f32[512,512]{0,1:T(8,128)S(1)}, f32[512,512]{0,1:T(8,128)}, u32[]{:S(2)}) copy-start(f32[512,512]{0,1:T(8,128)} %div.41) | copy-start | bytes 3145732
  171.4 16.2 %collective-permute-start.9 = (f32[128,512]{1,0:T(8,128)S(1)}, f32[128,512]{1,0:T(8,128)S(1)}, u32[]{:S(2)}, u32[]{:S(2)}) collective-permute-start(f32[128,512]{1,0:T(8,128)S(1)} %constant_dynamic-slice_fusion.3), channel_id=1, source_target_pairs={{0,8},{8,0},{1,9},{9,1},{2,10},{10,2},{3,11},{11,3},{4,12},{12,4},... | collective-permute-start | bytes 786440 | tf_op jit(solution)/shard_map/ppermute | solution.py:64
  173.3 17.7 %copy-start.12 = (bf16[512,512]{0,1:T(8,128)(2,1)S(1)}, bf16[512,512]{0,1:T(8,128)(2,1)}, u32[]{:S(2)}) copy-start(bf16[512,512]{0,1:T(8,128)(2,1)} %copy.30) | copy-start | bytes 1572868
  173.4 17.7 %copy-start.13 = (bf16[256,2,512]{2,1,0:T(2,128)(2,1)S(1)}, bf16[256,2,512]{2,1,0:T(2,128)(2,1)}, u32[]{:S(2)}) copy-start(bf16[256,2,512]{2,1,0:T(2,128)(2,1)} %dot_general.46) | copy-start | bytes 1572868
  187.7 16.1 %collective-permute-start.10 = (f32[64,512]{1,0:T(8,128)S(1)}, f32[64,512]{1,0:T(8,128)S(1)}, u32[]{:S(2)}, u32[]{:S(2)}) collective-permute-start(f32[64,512]{1,0:T(8,128)S(1)} %constant_dynamic-slice_fusion.2), channel_id=1, source_target_pairs={{0,16},{16,0},{1,17},{17,1},{2,18},{18,2},{3,19},{19,3},{4,20},{20... | collective-permute-start | bytes 393224 | tf_op jit(solution)/shard_map/ppermute | solution.py:64
  203.8 6.2 %collective-permute-start.11 = (f32[32,512]{1,0:T(8,128)S(1)}, f32[32,512]{1,0:T(8,128)S(1)}, u32[]{:S(2)}, u32[]{:S(2)}) collective-permute-start(f32[32,512]{1,0:T(8,128)S(1)} %constant_dynamic-slice_fusion.1), channel_id=1, source_target_pairs={{0,1},{1,0},{2,3},{3,2},{4,5},{5,4},{6,7},{7,6},{8,9},{9,8},{10,11... | collective-permute-start | bytes 196616 | tf_op jit(solution)/shard_map/ppermute | solution.py:64
  207.3 10.3 %copy-start.14 = (f32[256,16]{0,1:T(8,128)}, f32[256,16]{0,1:T(8,128)S(1)}, u32[]{:S(2)}) copy-start(f32[256,16]{0,1:T(8,128)S(1)} %broadcast_add_fusion.2) | copy-start | bytes 49156
  210.0 14.4 %collective-permute-start.12 = (f32[16,512]{1,0:T(8,128)S(1)}, f32[16,512]{1,0:T(8,128)S(1)}, u32[]{:S(2)}, u32[]{:S(2)}) collective-permute-start(f32[16,512]{1,0:T(8,128)S(1)} %constant_dynamic-slice_fusion), channel_id=1, source_target_pairs={{0,2},{2,0},{1,3},{3,1},{4,6},{6,4},{5,7},{7,5},{8,10},{10,8},{9,1... | collective-permute-start | bytes 98312 | tf_op jit(solution)/shard_map/ppermute | solution.py:64

commit v3 on v2

--- a/solution.py
+++ b/solution.py
@@ -5,14 +5,22 @@
 from jax.sharding import Mesh
 from jax.sharding import PartitionSpec as P
 
-PIPE_MODE = "ppermute"
-TENSOR_MODE = "ppermute"
+X_MODE = "direct"
+Y_MODE = "direct"
 
-FINE = ("z_hi", "x2", "x1", "core", "z4", "z2", "z1", "y2", "y1")
-PIPE = ("z_hi", "x2", "x1", "core")
-TENSOR = ("z4", "z2", "z1", "y2", "y1")
-PIPE_STAGES = ("core", "x1", "x2", "z_hi")
-TENSOR_STAGES = ("z1", "z2", "z4", "y1", "y2")
+if X_MODE == "direct":
+    PIPE = ("z_hi", "x", "core")
+    PIPE_STAGES = ("core", "x", "z_hi")
+else:
+    PIPE = ("z_hi", "x2", "x1", "core")
+    PIPE_STAGES = ("core", "x1", "x2", "z_hi")
+if Y_MODE == "direct":
+    TENSOR = ("z4", "z2", "z1", "y")
+    TENSOR_STAGES = ("y", "z1", "z2", "z4")
+else:
+    TENSOR = ("z4", "z2", "z1", "y2", "y1")
+    TENSOR_STAGES = ("z1", "z2", "z4", "y1", "y2")
+FINE = PIPE + TENSOR
 
 
 def quantize_features(grad):
@@ -54,54 +62,59 @@
     return (hidden, gate_grad, up_grad)
 
 
-def halve(x, axis, dim, mode):
-    if mode == "xla":
-        return lax.psum_scatter(x, axis, scatter_dimension=dim, tiled=True)
-    half = x.shape[dim] // 2
+def scatter_sum(x, axis, dim):
+    n = lax.psum(1, axis)
+    size = x.shape[dim] // n
     me = lax.axis_index(axis)
-    keep = lax.dynamic_slice_in_dim(x, me * half, half, axis=dim)
-    send = lax.dynamic_slice_in_dim(x, (1 - me) * half, half, axis=dim)
-    return keep + lax.ppermute(send, axis, perm=[(0, 1), (1, 0)])
+    acc = lax.dynamic_slice_in_dim(x, me * size, size, axis=dim)
+    for shift in range(1, n):
+        send = lax.dynamic_slice_in_dim(x, ((me + shift) % n) * size, size, axis=dim)
+        perm = [(j, (j + shift) % n) for j in range(n)]
+        acc = acc + lax.ppermute(send, axis, perm=perm)
+    return acc
 
 
-def double(x, axis, dim, mode):
-    if mode == "xla":
-        return lax.all_gather(x, axis, axis=dim, tiled=True)
+def gather(x, axis, dim):
+    n = lax.psum(1, axis)
+    size = x.shape[dim]
     me = lax.axis_index(axis)
-    other = lax.ppermute(x, axis, perm=[(0, 1), (1, 0)])
-    both = jnp.concatenate([other, other], axis=dim)
-    return lax.dynamic_update_slice_in_dim(both, x, me * x.shape[dim], axis=dim)
+    full = jnp.concatenate([x] * n, axis=dim)
+    for shift in range(1, n):
+        perm = [(j, (j + shift) % n) for j in range(n)]
+        got = lax.ppermute(x, axis, perm=perm)
+        full = lax.dynamic_update_slice_in_dim(full, got, ((me - shift) % n) * size, axis=dim)
+    return full
 
 
 def pipe_exchange(parts):
     shard = jnp.stack(parts)
     for axis in PIPE_STAGES:
-        shard = halve(shard, axis, 1, PIPE_MODE)
+        shard = scatter_sum(shard, axis, 1)
     full = jnp.stack(gate_terms(shard[0], shard[1], shard[2]))
     for axis in reversed(PIPE_STAGES):
-        full = double(full, axis, 1, PIPE_MODE)
+        full = gather(full, axis, 1)
     return full[0], full[1], full[2]
 
 
-def tensor_exchange(partial):
+def tensor_exchange(partial, sizes):
     rows, cols = partial.shape
-    bits = len(TENSOR)
-    blocks = partial.reshape((2,) * bits + (rows >> bits, cols))
+    count = len(TENSOR)
+    blocks = partial.reshape(tuple(sizes[a] for a in TENSOR) + (-1, cols))
     order = [TENSOR.index(a) for a in TENSOR_STAGES]
-    blocks = jnp.transpose(blocks, order + [bits, bits + 1]).reshape(rows, cols)
+    blocks = jnp.transpose(blocks, order + [count, count + 1]).reshape(rows, cols)
     for axis in TENSOR_STAGES:
-        blocks = halve(blocks, axis, 0, TENSOR_MODE)
+        blocks = scatter_sum(blocks, axis, 0)
     return blocks
 
 
-def make_on_device():
+def make_on_device(sizes):
     def on_device(tokens, out_grad, w_gate, w_up, w_down):
         gate_part = jnp.dot(tokens, w_gate, preferred_element_type=jnp.float32)
         up_part = jnp.dot(tokens, w_up, preferred_element_type=jnp.float32)
         hidden_part = contract_last(out_grad, w_down)
         hidden, gate_grad, up_grad = pipe_exchange((gate_part, up_part, hidden_part))
         input_grad = tensor_exchange(
-            contract_last(gate_grad, w_gate) + contract_last(up_grad, w_up)
+            contract_last(gate_grad, w_gate) + contract_last(up_grad, w_up), sizes
         )
         gate_mantissa, gate_scales = quantize_features(contract_first(tokens, gate_grad))
         up_mantissa, up_scales = quantize_features(contract_first(tokens, up_grad))
@@ -122,12 +135,15 @@
 def fine_mesh(mesh):
     n_pipe, n_tensor = mesh.shape["pipe"], mesh.shape["tensor"]
     assert n_pipe == 16 and n_tensor == 32
-    devices = np.asarray(mesh.devices).reshape((2,) * len(FINE))
-    return Mesh(devices, FINE)
+    sizes = {"z_hi": 2, "x": 4, "core": 2, "y": 4}
+    for axis in FINE:
+        sizes.setdefault(axis, 2)
+    devices = np.asarray(mesh.devices).reshape(tuple(sizes[a] for a in FINE))
+    return Mesh(devices, FINE), sizes
 
 
 def solution(mesh):
-    fine = fine_mesh(mesh)
+    fine, sizes = fine_mesh(mesh)
     in_specs = (
         P(None, PIPE),
         P(None, PIPE),
@@ -145,7 +161,7 @@
         P(TENSOR, PIPE),
     )
     return jax.shard_map(
-        make_on_device(),
+        make_on_device(sizes),
         mesh=fine,
         in_specs=in_specs,
         out_specs=out_specs,

time: 226 us -> 194 us (0.86)
  waiting for transfers between devices: 94.7 us -> 48.9 us
  starting transfers between devices: 65.3 us -> 81.3 us
  local copies, waits for them, and re-layouts: 39.8 us -> 37.5 us
    ppermute x13 -> x16, waiting for transfers between devices: 94.7 us -> 48.9 us  [the longest x11 30.6 us: scatter_sum(): acc = acc + lax.ppermute(send, axis, perm=perm)]
    ppermute x13 -> x16, starting transfers between devices: 65.3 us -> 81.3 us  [the longest x11 56.8 us: scatter_sum(): acc = acc + lax.ppermute(send, axis, perm=perm)]
    unnamed x35 -> x31, local copies, waits for them, and re-layouts: 9.44 us -> 9.2 us
    add x9 -> x7, other arithmetic: 5.39 us -> 5.56 us  [scatter_sum(): acc = acc + lax.ppermute(send, axis, perm=perm)]
  transfers between devices with their start and end apart: 13 -> 16, of which waited for: 11 -> 12; matrix products, arithmetic and copies ran while one was open for 18% -> 20% of each run, Pallas kernels for 0% -> 0%
where the time goes in v3:
time: 194 us; the launch traced here: 192 us
  starting transfers between devices  81.3 us (42%)
  waiting for transfers between devices  48.9 us (25%)
  local copies, waits for them, and re-layouts  37.5 us (19%)
  other arithmetic  14.4 us (7%)
  matrix products  8.77 us (5%)
    ppermute x11, starting transfers between devices, scatter_sum(): acc = acc + lax.ppermute(send, axis, perm=perm)  56.8 us
    ppermute x11, waiting for transfers between devices, scatter_sum(): acc = acc + lax.ppermute(send, axis, perm=perm)  30.6 us
    ppermute x5, starting transfers between devices, gather(): got = lax.ppermute(x, axis, perm=perm)  24.5 us
    ppermute x5, waiting for transfers between devices, gather(): got = lax.ppermute(x, axis, perm=perm)  18.3 us
    div x4, local copies, waits for them, and re-layouts, quantize_features(): mantissa = (blocks / scales[:, None, :, None]).reshape(grad.shape)  13 us
    unnamed x31, local copies, waits for them, and re-layouts  9.2 us
    convert_element_type x2, local copies, waits for them, and re-layouts, quantize_hidden(): return (mantissa.astype(jnp.bfloat16), scales)  5.75 us
    reduce_max x2, other arithmetic, quantize_features(): scales = jnp.max(jnp.abs(blocks), axis=(1, 3)) + 1e-06  5.62 us
  transfers between devices with their start and end apart: 16, of which 12 were waited for; matrix products, arithmetic and copies ran while one was open for 20% of the time, Pallas kernels for 0%

profile of v3, /device:TPU:6, one launch (start us, length us, event | category | flops | bytes accessed | tf_op | source)
XLA Modules:
  0.0 192.3 jit_solution(7003528655581326282)
XLA Ops:
  4.3 2.5 %convolution_bitcast_fusion.2 = f32[1,512,512]{2,1,0:T(8,128)} fusion(bf16[512,512]{1,0:T(8,128)(2,1)S(1)} %copy-done.7, bf16[512,512]{1,0:T(8,128)(2,1)} %param.9), kind=kOutput, calls=%fused_computation.6 | convolution fusion | flops 268435456 | bytes 2097152 | tf_op jit(solution)/shard_map/dot_general | solution.py:43
  11.9 3.5 %collective-permute-done = f32[3,256,512]{2,1,0:T(8,128)} collective-permute-done((f32[3,256,512]{2,1,0:T(8,128)S(1)}, f32[3,256,512]{2,1,0:T(8,128)}, u32[]{:S(2)}, u32[]{:S(2)}) %collective-permute-start) | collective-permute-done | bytes 1572896 | tf_op jit(solution)/shard_map/ppermute | solution.py:73
  18.5 2.7 %collective-permute-start.3 = (f32[3,64,512]{2,1,0:T(8,128)}, f32[3,64,512]{2,1,0:T(8,128)}, u32[]{:S(2)}, u32[]{:S(2)}) collective-permute-start(f32[3,64,512]{2,1,0:T(8,128)} %get-tuple-element.29), channel_id=1, source_target_pairs={{0,192},{64,0},{128,64},{192,128},{1,193},{65,1},{129,65},{193,129... | collective-permute-start | bytes 1179656 | tf_op jit(solution)/shard_map/ppermute | solution.py:73
  21.2 8.4 %collective-permute-start.2 = (f32[3,64,512]{2,1,0:T(8,128)S(1)}, f32[3,64,512]{2,1,0:T(8,128)}, u32[]{:S(2)}, u32[]{:S(2)}) collective-permute-start(f32[3,64,512]{2,1,0:T(8,128)S(1)} %get-tuple-element.30), channel_id=1, source_target_pairs={{0,128},{64,192},{128,0},{192,64},{1,129},{65,193},{129,1},{193,65... | collective-permute-start | bytes 1179656 | tf_op jit(solution)/shard_map/ppermute | solution.py:73
  31.5 4.4 %collective-permute-done.3 = f32[3,64,512]{2,1,0:T(8,128)} collective-permute-done((f32[3,64,512]{2,1,0:T(8,128)}, f32[3,64,512]{2,1,0:T(8,128)}, u32[]{:S(2)}, u32[]{:S(2)}) %collective-permute-start.3) | collective-permute-done | bytes 393248 | tf_op jit(solution)/shard_map/ppermute | solution.py:73
  35.9 9.6 %collective-permute-done.2 = f32[3,64,512]{2,1,0:T(8,128)} collective-permute-done((f32[3,64,512]{2,1,0:T(8,128)S(1)}, f32[3,64,512]{2,1,0:T(8,128)}, u32[]{:S(2)}, u32[]{:S(2)}) %collective-permute-start.2) | collective-permute-done | bytes 393248 | tf_op jit(solution)/shard_map/ppermute | solution.py:73
  48.1 12.8 %collective-permute-start.4 = (f32[3,32,512]{2,1,0:T(8,128)S(1)}, f32[3,32,512]{2,1,0:T(8,128)S(1)}, u32[]{:S(2)}, u32[]{:S(2)}) collective-permute-start(f32[3,32,512]{2,1,0:T(8,128)S(1)} %constant_dynamic-slice_fusion.6), channel_id=1, source_target_pairs={{0,256},{256,0},{1,257},{257,1},{2,258},{258,2},{3,259},{259,3},{4... | collective-permute-start | bytes 589832 | tf_op jit(solution)/shard_map/ppermute | solution.py:73
  61.0 4.3 %collective-permute-done.4 = f32[3,32,512]{2,1,0:T(8,128)S(1)} collective-permute-done((f32[3,32,512]{2,1,0:T(8,128)S(1)}, f32[3,32,512]{2,1,0:T(8,128)S(1)}, u32[]{:S(2)}, u32[]{:S(2)}) %collective-permute-start.4) | collective-permute-done | bytes 196640 | tf_op jit(solution)/shard_map/ppermute | solution.py:73
  65.4 12.3 %collective-permute-start.5 = (bf16[3,32,512]{2,1,0:T(8,128)(2,1)S(1)}, bf16[3,32,512]{2,1,0:T(8,128)(2,1)S(1)}, u32[]{:S(2)}, u32[]{:S(2)}) collective-permute-start(bf16[3,32,512]{2,1,0:T(8,128)(2,1)S(1)} %pad_maximum_fusion.3), channel_id=1, source_target_pairs={{0,256},{256,0},{1,257},{257,1},{2,258},{258,2},{3,259},{259,3},{4... | collective-permute-start | bytes 294920 | tf_op jit(solution)/shard_map/ppermute | solution.py:84
  77.8 8.1 %collective-permute-done.5 = bf16[3,32,512]{2,1,0:T(8,128)(2,1)S(1)} collective-permute-done((bf16[3,32,512]{2,1,0:T(8,128)(2,1)S(1)}, bf16[3,32,512]{2,1,0:T(8,128)(2,1)S(1)}, u32[]{:S(2)}, u32[]{:S(2)}) %collective-permute-start.5) | collective-permute-done | bytes 98336 | tf_op jit(solution)/shard_map/ppermute | solution.py:84
  85.9 5.6 %collective-permute-start.6 = (bf16[3,64,512]{2,1,0:T(8,128)(2,1)S(1)}, bf16[3,64,512]{2,1,0:T(8,128)(2,1)S(1)}, u32[]{:S(2)}, u32[]{:S(2)}) collective-permute-start(bf16[3,64,512]{2,1,0:T(8,128)(2,1)S(1)} %constant_dynamic-update-slice_fusion.4), channel_id=1, source_target_pairs={{0,64},{64,128},{128,192},{192,0},{1,65},{65,129},{129,193},{193,1... | collective-permute-start | bytes 589832 | tf_op jit(solution)/shard_map/ppermute | solution.py:84
  93.6 2.6 %collective-permute-start.8 = (bf16[3,64,512]{2,1,0:T(8,128)(2,1)S(1)}, bf16[3,64,512]{2,1,0:T(8,128)(2,1)S(1)}, u32[]{:S(2)}, u32[]{:S(2)}) collective-permute-start(bf16[3,64,512]{2,1,0:T(8,128)(2,1)S(1)} %constant_dynamic-update-slice_fusion.4), channel_id=1, source_target_pairs={{0,192},{64,0},{128,64},{192,128},{1,193},{65,1},{129,65},{193,129... | collective-permute-start | bytes 589832 | tf_op jit(solution)/shard_map/ppermute | solution.py:84
  96.3 3.6 %collective-permute-done.6 = bf16[3,64,512]{2,1,0:T(8,128)(2,1)S(1)} collective-permute-done((bf16[3,64,512]{2,1,0:T(8,128)(2,1)S(1)}, bf16[3,64,512]{2,1,0:T(8,128)(2,1)S(1)}, u32[]{:S(2)}, u32[]{:S(2)}) %collective-permute-start.6) | collective-permute-done | bytes 196640 | tf_op jit(solution)/shard_map/ppermute | solution.py:84
  99.9 2.8 %collective-permute-done.7 = bf16[3,64,512]{2,1,0:T(8,128)(2,1)S(1)} collective-permute-done((bf16[3,64,512]{2,1,0:T(8,128)(2,1)S(1)}, bf16[3,64,512]{2,1,0:T(8,128)(2,1)S(1)}, u32[]{:S(2)}, u32[]{:S(2)}) %collective-permute-start.7) | collective-permute-done | bytes 196640 | tf_op jit(solution)/shard_map/ppermute | solution.py:84
  102.7 2.8 %collective-permute-done.8 = bf16[3,64,512]{2,1,0:T(8,128)(2,1)S(1)} collective-permute-done((bf16[3,64,512]{2,1,0:T(8,128)(2,1)S(1)}, bf16[3,64,512]{2,1,0:T(8,128)(2,1)S(1)}, u32[]{:S(2)}, u32[]{:S(2)}) %collective-permute-start.8) | collective-permute-done | bytes 196640 | tf_op jit(solution)/shard_map/ppermute | solution.py:84
  115.7 4.9 %collective-permute-start.12 = (f32[128,512]{1,0:T(8,128)}, f32[128,512]{1,0:T(8,128)}, u32[]{:S(2)}, u32[]{:S(2)}) collective-permute-start(f32[128,512]{1,0:T(8,128)} %get-tuple-element.32), channel_id=1, source_target_pairs={{0,3},{1,0},{2,1},{3,2},{4,7},{5,4},{6,5},{7,6},{8,11},{9,8},{10,9... | collective-permute-start | bytes 786440 | tf_op jit(solution)/shard_map/ppermute | solution.py:73
  120.6 2.5 %collective-permute-start.11 = (f32[128,512]{1,0:T(8,128)}, f32[128,512]{1,0:T(8,128)}, u32[]{:S(2)}, u32[]{:S(2)}) collective-permute-start(f32[128,512]{1,0:T(8,128)} %get-tuple-element.33), channel_id=1, source_target_pairs={{0,2},{1,3},{2,0},{3,1},{4,6},{5,7},{6,4},{7,5},{8,10},{9,11},{10,... | collective-permute-start | bytes 786440 | tf_op jit(solution)/shard_map/ppermute | solution.py:73
  123.2 2.9 %collective-permute-start.10 = (f32[128,512]{1,0:T(8,128)}, f32[128,512]{1,0:T(8,128)}, u32[]{:S(2)}, u32[]{:S(2)}) collective-permute-start(f32[128,512]{1,0:T(8,128)} %get-tuple-element.31), channel_id=1, source_target_pairs={{0,1},{1,2},{2,3},{3,0},{4,5},{5,6},{6,7},{7,4},{8,9},{9,10},{10,1... | collective-permute-start | bytes 786440 | tf_op jit(solution)/shard_map/ppermute | solution.py:73
  126.1 2.5 %abs.16 = f32[16,32,256,2]{1,0,3,2:T(8,128)} reshape(f32[512,512]{0,1:T(8,128)S(1)} %get-tuple-element.37) | data formatting | bytes 2097152 | tf_op jit(solution)/shard_map/abs | solution.py:29
  128.6 2.8 %reduce_max.27 = f32[16,256]{0,1:T(8,128)S(1)} reduce(f32[16,32,256,2]{1,0,3,2:T(8,128)} %abs.16, f32[]{:T(128)} %constant.135.clone.1), dimensions={1,3}, to_apply=%region_0.1 | reduce | flops 258048 | bytes 1064964 | tf_op jit(solution)/shard_map/reduce_max | solution.py:29
  131.4 2.5 %div.37 = f32[16,32,256,2]{1,0,3,2:T(8,128)} broadcast(f32[16,256]{0,1:T(8,128)S(1)} %broadcast_add_fusion.1), dimensions={0,2} | broadcast | bytes 1064960 | tf_op jit(solution)/shard_map/div | solution.py:30
  133.9 3.5 %div.38 = f32[512,512]{0,1:T(8,128)S(1)} reshape(f32[16,32,256,2]{1,0,3,2:T(8,128)} %div.37) | data formatting | bytes 2097152 | tf_op jit(solution)/shard_map/div | solution.py:30
  137.5 2.5 %abs.18 = f32[16,32,256,2]{1,0,3,2:T(8,128)} reshape(f32[512,512]{0,1:T(8,128)S(1)} %get-tuple-element.39) | data formatting | bytes 2097152 | tf_op jit(solution)/shard_map/abs | solution.py:29
  140.0 2.8 %reduce_max.28 = f32[16,256]{0,1:T(8,128)S(1)} reduce(f32[16,32,256,2]{1,0,3,2:T(8,128)} %abs.18, f32[]{:T(128)} %constant.135.clone.1), dimensions={1,3}, to_apply=%region_1.2 | reduce | flops 258048 | bytes 1064964 | tf_op jit(solution)/shard_map/reduce_max | solution.py:29
  142.8 2.5 %div.40 = f32[16,32,256,2]{1,0,3,2:T(8,128)} broadcast(f32[16,256]{0,1:T(8,128)S(1)} %broadcast_add_fusion), dimensions={0,2} | broadcast | bytes 1064960 | tf_op jit(solution)/shard_map/div | solution.py:30
  145.4 4.4 %div.41 = f32[512,512]{0,1:T(8,128)} reshape(f32[16,32,256,2]{1,0,3,2:T(8,128)} %div.40) | data formatting | bytes 2097152 | tf_op jit(solution)/shard_map/div | solution.py:30
  155.4 10.5 %collective-permute-start.13 = (f32[64,512]{1,0:T(8,128)S(1)}, f32[64,512]{1,0:T(8,128)S(1)}, u32[]{:S(2)}, u32[]{:S(2)}) collective-permute-start(f32[64,512]{1,0:T(8,128)S(1)} %constant_dynamic-slice_fusion.2), channel_id=1, source_target_pairs={{0,4},{4,0},{1,5},{5,1},{2,6},{6,2},{3,7},{7,3},{8,12},{12,8},{9,1... | collective-permute-start | bytes 393224 | tf_op jit(solution)/shard_map/ppermute | solution.py:73
  166.4 2.6 %collective-permute-done.13 = f32[64,512]{1,0:T(8,128)S(1)} collective-permute-done((f32[64,512]{1,0:T(8,128)S(1)}, f32[64,512]{1,0:T(8,128)S(1)}, u32[]{:S(2)}, u32[]{:S(2)}) %collective-permute-start.13) | collective-permute-done | bytes 131104 | tf_op jit(solution)/shard_map/ppermute | solution.py:73
  171.0 5.1 %collective-permute-done.14 = f32[32,512]{1,0:T(8,128)S(1)} collective-permute-done((f32[32,512]{1,0:T(8,128)S(1)}, f32[32,512]{1,0:T(8,128)S(1)}, u32[]{:S(2)}, u32[]{:S(2)}) %collective-permute-start.14) | collective-permute-done | bytes 65568 | tf_op jit(solution)/shard_map/ppermute | solution.py:73
  176.1 6.3 %collective-permute-start.15 = (f32[16,512]{1,0:T(8,128)S(1)}, f32[16,512]{1,0:T(8,128)S(1)}, u32[]{:S(2)}, u32[]{:S(2)}) collective-permute-start(f32[16,512]{1,0:T(8,128)S(1)} %constant_dynamic-slice_fusion), channel_id=1, source_target_pairs={{0,16},{16,0},{1,17},{17,1},{2,18},{18,2},{3,19},{19,3},{4,20},{20... | collective-permute-start | bytes 98312 | tf_op jit(solution)/shard_map/ppermute | solution.py:73
  185.9 3.0 %copy.32 = bf16[256,2,16,32]{3,2,1,0:T(8,128)(2,1)S(1)} copy(bf16[256,2,16,32]{0,3,2,1:T(8,128)(2,1)S(1)} %divide_convert_fusion) | data formatting | bytes 1048576 | tf_op jit(solution)/shard_map/convert_element_type | solution.py:39
  188.9 2.8 %convert_element_type.30 = bf16[512,512]{1,0:T(8,128)(2,1)} reshape(bf16[256,2,16,32]{3,2,1,0:T(8,128)(2,1)S(1)} %copy.32) | data formatting | bytes 1048576 | tf_op jit(solution)/shard_map/convert_element_type | solution.py:39
  (84 shorter events, 40.6 us)
Async XLA Ops:
  0.6 1.0 copy-start
  1.7 1.5 copy-start.9
  3.2 1.0 copy-start.7
  8.3 1.6 copy-start.1
  10.0 5.4 %collective-permute-start = (f32[3,256,512]{2,1,0:T(8,128)S(1)}, f32[3,256,512]{2,1,0:T(8,128)}, u32[]{:S(2)}, u32[]{:S(2)}) collective-permute-start(f32[3,256,512]{2,1,0:T(8,128)S(1)} %constant_dynamic-slice_fusion.10), channel_id=1, source_target_pairs={{0,32},{32,0},{1,33},{33,1},{2,34},{34,2},{3,35},{35,3},{4,36},{36... | collective-permute-start | bytes 4718600 | tf_op jit(solution)/shard_map/ppermute | solution.py:73
  18.5 17.4 %collective-permute-start.3 = (f32[3,64,512]{2,1,0:T(8,128)}, f32[3,64,512]{2,1,0:T(8,128)}, u32[]{:S(2)}, u32[]{:S(2)}) collective-permute-start(f32[3,64,512]{2,1,0:T(8,128)} %get-tuple-element.29), channel_id=1, source_target_pairs={{0,192},{64,0},{128,64},{192,128},{1,193},{65,1},{129,65},{193,129... | collective-permute-start | bytes 1179656 | tf_op jit(solution)/shard_map/ppermute | solution.py:73
  21.2 24.3 %collective-permute-start.2 = (f32[3,64,512]{2,1,0:T(8,128)S(1)}, f32[3,64,512]{2,1,0:T(8,128)}, u32[]{:S(2)}, u32[]{:S(2)}) collective-permute-start(f32[3,64,512]{2,1,0:T(8,128)S(1)} %get-tuple-element.30), channel_id=1, source_target_pairs={{0,128},{64,192},{128,0},{192,64},{1,129},{65,193},{129,1},{193,65... | collective-permute-start | bytes 1179656 | tf_op jit(solution)/shard_map/ppermute | solution.py:73
  29.6 17.1 %collective-permute-start.1 = (f32[3,64,512]{2,1,0:T(8,128)S(1)}, f32[3,64,512]{2,1,0:T(8,128)}, u32[]{:S(2)}, u32[]{:S(2)}) collective-permute-start(f32[3,64,512]{2,1,0:T(8,128)S(1)} %get-tuple-element.28), channel_id=1, source_target_pairs={{0,64},{64,128},{128,192},{192,0},{1,65},{65,129},{129,193},{193,1... | collective-permute-start | bytes 1179656 | tf_op jit(solution)/shard_map/ppermute | solution.py:73
  48.1 17.2 %collective-permute-start.4 = (f32[3,32,512]{2,1,0:T(8,128)S(1)}, f32[3,32,512]{2,1,0:T(8,128)S(1)}, u32[]{:S(2)}, u32[]{:S(2)}) collective-permute-start(f32[3,32,512]{2,1,0:T(8,128)S(1)} %constant_dynamic-slice_fusion.6), channel_id=1, source_target_pairs={{0,256},{256,0},{1,257},{257,1},{2,258},{258,2},{3,259},{259,3},{4... | collective-permute-start | bytes 589832 | tf_op jit(solution)/shard_map/ppermute | solution.py:73
  65.4 20.5 %collective-permute-start.5 = (bf16[3,32,512]{2,1,0:T(8,128)(2,1)S(1)}, bf16[3,32,512]{2,1,0:T(8,128)(2,1)S(1)}, u32[]{:S(2)}, u32[]{:S(2)}) collective-permute-start(bf16[3,32,512]{2,1,0:T(8,128)(2,1)S(1)} %pad_maximum_fusion.3), channel_id=1, source_target_pairs={{0,256},{256,0},{1,257},{257,1},{2,258},{258,2},{3,259},{259,3},{4... | collective-permute-start | bytes 294920 | tf_op jit(solution)/shard_map/ppermute | solution.py:84
  85.9 14.0 %collective-permute-start.6 = (bf16[3,64,512]{2,1,0:T(8,128)(2,1)S(1)}, bf16[3,64,512]{2,1,0:T(8,128)(2,1)S(1)}, u32[]{:S(2)}, u32[]{:S(2)}) collective-permute-start(bf16[3,64,512]{2,1,0:T(8,128)(2,1)S(1)} %constant_dynamic-update-slice_fusion.4), channel_id=1, source_target_pairs={{0,64},{64,128},{128,192},{192,0},{1,65},{65,129},{129,193},{193,1... | collective-permute-start | bytes 589832 | tf_op jit(solution)/shard_map/ppermute | solution.py:84
  91.5 11.2 %collective-permute-start.7 = (bf16[3,64,512]{2,1,0:T(8,128)(2,1)S(1)}, bf16[3,64,512]{2,1,0:T(8,128)(2,1)S(1)}, u32[]{:S(2)}, u32[]{:S(2)}) collective-permute-start(bf16[3,64,512]{2,1,0:T(8,128)(2,1)S(1)} %constant_dynamic-update-slice_fusion.4), channel_id=1, source_target_pairs={{0,128},{64,192},{128,0},{192,64},{1,129},{65,193},{129,1},{193,65... | collective-permute-start | bytes 589832 | tf_op jit(solution)/shard_map/ppermute | solution.py:84
  93.6 11.9 %collective-permute-start.8 = (bf16[3,64,512]{2,1,0:T(8,128)(2,1)S(1)}, bf16[3,64,512]{2,1,0:T(8,128)(2,1)S(1)}, u32[]{:S(2)}, u32[]{:S(2)}) collective-permute-start(bf16[3,64,512]{2,1,0:T(8,128)(2,1)S(1)} %constant_dynamic-update-slice_fusion.4), channel_id=1, source_target_pairs={{0,192},{64,0},{128,64},{192,128},{1,193},{65,1},{129,65},{193,129... | collective-permute-start | bytes 589832 | tf_op jit(solution)/shard_map/ppermute | solution.py:84
  105.6 4.2 %collective-permute-start.9 = (bf16[3,256,512]{2,1,0:T(8,128)(2,1)S(1)}, bf16[3,256,512]{2,1,0:T(8,128)(2,1)S(1)}, u32[]{:S(2)}, u32[]{:S(2)}) collective-permute-start(bf16[3,256,512]{2,1,0:T(8,128)(2,1)S(1)} %constant_dynamic-update-slice_fusion.1), channel_id=1, source_target_pairs={{0,32},{32,0},{1,33},{33,1},{2,34},{34,2},{3,35},{35,3},{4,36},{36... | collective-permute-start | bytes 2359304 | tf_op jit(solution)/shard_map/ppermute | solution.py:84
  108.6 1.2 copy-start.8
  111.7 1.5 copy-start.10
  113.8 1.0 copy-start.5
  115.7 38.3 %collective-permute-start.12 = (f32[128,512]{1,0:T(8,128)}, f32[128,512]{1,0:T(8,128)}, u32[]{:S(2)}, u32[]{:S(2)}) collective-permute-start(f32[128,512]{1,0:T(8,128)} %get-tuple-element.32), channel_id=1, source_target_pairs={{0,3},{1,0},{2,1},{3,2},{4,7},{5,4},{6,5},{7,6},{8,11},{9,8},{10,9... | collective-permute-start | bytes 786440 | tf_op jit(solution)/shard_map/ppermute | solution.py:73
  120.6 33.4 %collective-permute-start.11 = (f32[128,512]{1,0:T(8,128)}, f32[128,512]{1,0:T(8,128)}, u32[]{:S(2)}, u32[]{:S(2)}) collective-permute-start(f32[128,512]{1,0:T(8,128)} %get-tuple-element.33), channel_id=1, source_target_pairs={{0,2},{1,3},{2,0},{3,1},{4,6},{5,7},{6,4},{7,5},{8,10},{9,11},{10,... | collective-permute-start | bytes 786440 | tf_op jit(solution)/shard_map/ppermute | solution.py:73
  123.2 30.9 %collective-permute-start.10 = (f32[128,512]{1,0:T(8,128)}, f32[128,512]{1,0:T(8,128)}, u32[]{:S(2)}, u32[]{:S(2)}) collective-permute-start(f32[128,512]{1,0:T(8,128)} %get-tuple-element.31), channel_id=1, source_target_pairs={{0,1},{1,2},{2,3},{3,0},{4,5},{5,6},{6,7},{7,4},{8,9},{9,10},{10,1... | collective-permute-start | bytes 786440 | tf_op jit(solution)/shard_map/ppermute | solution.py:73
  149.8 2.3 %copy-start.3 = (f32[512,512]{0,1:T(8,128)S(1)}, f32[512,512]{0,1:T(8,128)}, u32[]{:S(2)}) copy-start(f32[512,512]{0,1:T(8,128)} %get-tuple-element.38) | copy-start | bytes 3145732
  152.0 1.4 copy-start.2
  152.1 1.7 copy-start.4
  153.8 12.1 %copy-start.11 = (bf16[512,512]{0,1:T(8,128)(2,1)S(1)}, bf16[512,512]{0,1:T(8,128)(2,1)}, u32[]{:S(2)}) copy-start(bf16[512,512]{0,1:T(8,128)(2,1)} %copy.30) | copy-start | bytes 1572868
  155.4 13.6 %collective-permute-start.13 = (f32[64,512]{1,0:T(8,128)S(1)}, f32[64,512]{1,0:T(8,128)S(1)}, u32[]{:S(2)}, u32[]{:S(2)}) collective-permute-start(f32[64,512]{1,0:T(8,128)S(1)} %constant_dynamic-slice_fusion.2), channel_id=1, source_target_pairs={{0,4},{4,0},{1,5},{5,1},{2,6},{6,2},{3,7},{7,3},{8,12},{12,8},{9,1... | collective-permute-start | bytes 393224 | tf_op jit(solution)/shard_map/ppermute | solution.py:73
  166.4 17.5 %copy-start.6 = (bf16[512,512]{0,1:T(8,128)(2,1)S(1)}, bf16[512,512]{0,1:T(8,128)(2,1)}, u32[]{:S(2)}) copy-start(bf16[512,512]{0,1:T(8,128)(2,1)} %divide_convert_fusion.2) | copy-start | bytes 1572868
  169.0 7.1 %collective-permute-start.14 = (f32[32,512]{1,0:T(8,128)S(1)}, f32[32,512]{1,0:T(8,128)S(1)}, u32[]{:S(2)}, u32[]{:S(2)}) collective-permute-start(f32[32,512]{1,0:T(8,128)S(1)} %constant_dynamic-slice_fusion.1), channel_id=1, source_target_pairs={{0,8},{8,0},{1,9},{9,1},{2,10},{10,2},{3,11},{11,3},{4,12},{12,4},... | collective-permute-start | bytes 196616 | tf_op jit(solution)/shard_map/ppermute | solution.py:73
  171.0 13.9 %copy-start.12 = (f32[256,16]{0,1:T(8,128)}, f32[256,16]{0,1:T(8,128)S(1)}, u32[]{:S(2)}) copy-start(f32[256,16]{0,1:T(8,128)S(1)} %broadcast_add_fusion.2) | copy-start | bytes 49156
  176.1 15.5 %collective-permute-start.15 = (f32[16,512]{1,0:T(8,128)S(1)}, f32[16,512]{1,0:T(8,128)S(1)}, u32[]{:S(2)}, u32[]{:S(2)}) collective-permute-start(f32[16,512]{1,0:T(8,128)S(1)} %constant_dynamic-slice_fusion), channel_id=1, source_target_pairs={{0,16},{16,0},{1,17},{17,1},{2,18},{18,2},{3,19},{19,3},{4,20},{20... | collective-permute-start | bytes 98312 | tf_op jit(solution)/shard_map/ppermute | solution.py:73

commit v4 on v3

--- a/solution.py
+++ b/solution.py
@@ -37,6 +37,10 @@
     scales = jnp.max(jnp.abs(blocks), axis=(1, 3)) + 1e-06
     mantissa = (blocks / scales[:, None, :, None]).reshape(grad.shape)
     return (mantissa.astype(jnp.bfloat16), scales)
+
+
+def transposed(pair):
+    return (pair[0].T, pair[1].T)
 
 
 def contract_last(left, right):
@@ -116,8 +120,8 @@
         input_grad = tensor_exchange(
             contract_last(gate_grad, w_gate) + contract_last(up_grad, w_up), sizes
         )
-        gate_mantissa, gate_scales = quantize_features(contract_first(tokens, gate_grad))
-        up_mantissa, up_scales = quantize_features(contract_first(tokens, up_grad))
+        gate_mantissa, gate_scales = transposed(quantize_hidden(contract_first(gate_grad, tokens)))
+        up_mantissa, up_scales = transposed(quantize_hidden(contract_first(up_grad, tokens)))
         down_mantissa, down_scales = quantize_hidden(contract_first(hidden, out_grad))
         return (
             input_grad,

time: 194 us -> 188 us (0.969)
  other arithmetic: 14.4 us -> 10.5 us
  local copies, waits for them, and re-layouts: 37.5 us -> 34.5 us
  waiting for transfers between devices: 48.9 us -> 51.1 us
    div x4 -> x0, local copies, waits for them, and re-layouts: 13 us -> none  [quantize_features(): mantissa = (blocks / scales[:, None, :, None]).reshape(grad.shape)]
    convert_element_type x2 -> x6, local copies, waits for them, and re-layouts: 5.75 us -> 17.3 us  [quantize_hidden(): return (mantissa.astype(jnp.bfloat16), scales)]
    reduce_max x2 -> x0, other arithmetic: 5.62 us -> none  [quantize_features(): scales = jnp.max(jnp.abs(blocks), axis=(1, 3)) + 1e-06]
    abs x2 -> x0, local copies, waits for them, and re-layouts: 5.02 us -> none  [quantize_features(): scales = jnp.max(jnp.abs(blocks), axis=(1, 3)) + 1e-06]
    dot_general x3 -> x7, local copies, waits for them, and re-layouts: 2.28 us -> 5.61 us  [contract_first(): lax.dot_general(left, right, (((0,), (0,)), ((), ())), preferred_element_...]
    ppermute x11, waiting for transfers between devices: 30.6 us -> 33.8 us  [scatter_sum(): acc = acc + lax.ppermute(send, axis, perm=perm)]
    unnamed x31 -> x30, local copies, waits for them, and re-layouts: 9.2 us -> 9.44 us
  transfers between devices with their start and end apart: 16 -> 16, of which waited for: 12 -> 12; matrix products, arithmetic and copies ran while one was open for 20% -> 18% of each run, Pallas kernels for 0% -> 0%
where the time goes in v4:
time: 188 us; the launch traced here: 187 us
  starting transfers between devices  81.5 us (43%)
  waiting for transfers between devices  51.1 us (27%)
  local copies, waits for them, and re-layouts  34.5 us (18%)
  other arithmetic  10.5 us (6%)
  matrix products  8.12 us (4%)
    ppermute x11, starting transfers between devices, scatter_sum(): acc = acc + lax.ppermute(send, axis, perm=perm)  56.9 us
    ppermute x11, waiting for transfers between devices, scatter_sum(): acc = acc + lax.ppermute(send, axis, perm=perm)  33.8 us
    ppermute x5, starting transfers between devices, gather(): got = lax.ppermute(x, axis, perm=perm)  24.6 us
    ppermute x5, waiting for transfers between devices, gather(): got = lax.ppermute(x, axis, perm=perm)  17.3 us
    convert_element_type x6, local copies, waits for them, and re-layouts, quantize_hidden(): return (mantissa.astype(jnp.bfloat16), scales)  17.3 us
    unnamed x30, local copies, waits for them, and re-layouts  9.44 us
    dot_general x7, local copies, waits for them, and re-layouts, contract_first(): lax.dot_general(left, right, (((0,), (0,)), ((), ())), preferred_element_...  5.61 us
    add x7, other arithmetic, scatter_sum(): acc = acc + lax.ppermute(send, axis, perm=perm)  5.47 us
  transfers between devices with their start and end apart: 16, of which 12 were waited for; matrix products, arithmetic and copies ran while one was open for 18% of the time, Pallas kernels for 0%

profile of v4, /device:TPU:6, one launch (start us, length us, event | category | flops | bytes accessed | tf_op | source)
XLA Modules:
  0.0 187.1 jit_solution(10675825795903025155)
XLA Ops:
  3.7 2.7 %convolution_bitcast_fusion = f32[1,512,512]{2,1,0:T(8,128)} fusion(bf16[512,512]{1,0:T(8,128)(2,1)} %param.6, bf16[512,512]{1,0:T(8,128)(2,1)} %param.9), kind=kOutput, calls=%fused_computation.4 | convolution fusion | flops 268435456 | bytes 2097152 | tf_op jit(solution)/shard_map/dot_general | solution.py:47
  11.5 3.5 %collective-permute-done = f32[3,256,512]{2,1,0:T(8,128)} collective-permute-done((f32[3,256,512]{2,1,0:T(8,128)S(1)}, f32[3,256,512]{2,1,0:T(8,128)}, u32[]{:S(2)}, u32[]{:S(2)}) %collective-permute-start) | collective-permute-done | bytes 1572896 | tf_op jit(solution)/shard_map/ppermute | solution.py:77
  14.9 2.2 %dynamic-slice_add_fusion = f32[3,256,512]{2,1,0:T(8,128)S(1)} fusion(f32[3,256,512]{2,1,0:T(8,128)} %collective-permute-done, f32[3,512,512]{2,1,0:T(8,128)} %copy-done.1, s32[]{:T(128)S(6)} %select_n.136), kind=kLoop, calls=%fused_computation.2 | loop fusion | flops 393216 | bytes 4718596 | tf_op jit(solution)/shard_map/add | solution.py:77
  18.0 2.7 %collective-permute-start.3 = (f32[3,64,512]{2,1,0:T(8,128)}, f32[3,64,512]{2,1,0:T(8,128)}, u32[]{:S(2)}, u32[]{:S(2)}) collective-permute-start(f32[3,64,512]{2,1,0:T(8,128)} %get-tuple-element.18), channel_id=1, source_target_pairs={{0,192},{64,0},{128,64},{192,128},{1,193},{65,1},{129,65},{193,129... | collective-permute-start | bytes 1179656 | tf_op jit(solution)/shard_map/ppermute | solution.py:77
  20.8 8.4 %collective-permute-start.2 = (f32[3,64,512]{2,1,0:T(8,128)S(1)}, f32[3,64,512]{2,1,0:T(8,128)}, u32[]{:S(2)}, u32[]{:S(2)}) collective-permute-start(f32[3,64,512]{2,1,0:T(8,128)S(1)} %get-tuple-element.19), channel_id=1, source_target_pairs={{0,128},{64,192},{128,0},{192,64},{1,129},{65,193},{129,1},{193,65... | collective-permute-start | bytes 1179656 | tf_op jit(solution)/shard_map/ppermute | solution.py:77
  31.1 4.4 %collective-permute-done.3 = f32[3,64,512]{2,1,0:T(8,128)} collective-permute-done((f32[3,64,512]{2,1,0:T(8,128)}, f32[3,64,512]{2,1,0:T(8,128)}, u32[]{:S(2)}, u32[]{:S(2)}) %collective-permute-start.3) | collective-permute-done | bytes 393248 | tf_op jit(solution)/shard_map/ppermute | solution.py:77
  35.5 9.6 %collective-permute-done.2 = f32[3,64,512]{2,1,0:T(8,128)} collective-permute-done((f32[3,64,512]{2,1,0:T(8,128)S(1)}, f32[3,64,512]{2,1,0:T(8,128)}, u32[]{:S(2)}, u32[]{:S(2)}) %collective-permute-start.2) | collective-permute-done | bytes 393248 | tf_op jit(solution)/shard_map/ppermute | solution.py:77
  47.7 12.8 %collective-permute-start.4 = (f32[3,32,512]{2,1,0:T(8,128)S(1)}, f32[3,32,512]{2,1,0:T(8,128)S(1)}, u32[]{:S(2)}, u32[]{:S(2)}) collective-permute-start(f32[3,32,512]{2,1,0:T(8,128)S(1)} %constant_dynamic-slice_fusion.6), channel_id=1, source_target_pairs={{0,256},{256,0},{1,257},{257,1},{2,258},{258,2},{3,259},{259,3},{4... | collective-permute-start | bytes 589832 | tf_op jit(solution)/shard_map/ppermute | solution.py:77
  60.5 4.3 %collective-permute-done.4 = f32[3,32,512]{2,1,0:T(8,128)S(1)} collective-permute-done((f32[3,32,512]{2,1,0:T(8,128)S(1)}, f32[3,32,512]{2,1,0:T(8,128)S(1)}, u32[]{:S(2)}, u32[]{:S(2)}) %collective-permute-start.4) | collective-permute-done | bytes 196640 | tf_op jit(solution)/shard_map/ppermute | solution.py:77
  65.0 12.3 %collective-permute-start.5 = (bf16[3,32,512]{2,1,0:T(8,128)(2,1)S(1)}, bf16[3,32,512]{2,1,0:T(8,128)(2,1)S(1)}, u32[]{:S(2)}, u32[]{:S(2)}) collective-permute-start(bf16[3,32,512]{2,1,0:T(8,128)(2,1)S(1)} %pad_maximum_fusion.3), channel_id=1, source_target_pairs={{0,256},{256,0},{1,257},{257,1},{2,258},{258,2},{3,259},{259,3},{4... | collective-permute-start | bytes 294920 | tf_op jit(solution)/shard_map/ppermute | solution.py:88
  77.3 8.1 %collective-permute-done.5 = bf16[3,32,512]{2,1,0:T(8,128)(2,1)S(1)} collective-permute-done((bf16[3,32,512]{2,1,0:T(8,128)(2,1)S(1)}, bf16[3,32,512]{2,1,0:T(8,128)(2,1)S(1)}, u32[]{:S(2)}, u32[]{:S(2)}) %collective-permute-start.5) | collective-permute-done | bytes 98336 | tf_op jit(solution)/shard_map/ppermute | solution.py:88
  85.4 5.6 %collective-permute-start.6 = (bf16[3,64,512]{2,1,0:T(8,128)(2,1)S(1)}, bf16[3,64,512]{2,1,0:T(8,128)(2,1)S(1)}, u32[]{:S(2)}, u32[]{:S(2)}) collective-permute-start(bf16[3,64,512]{2,1,0:T(8,128)(2,1)S(1)} %constant_dynamic-update-slice_fusion.4), channel_id=1, source_target_pairs={{0,64},{64,128},{128,192},{192,0},{1,65},{65,129},{129,193},{193,1... | collective-permute-start | bytes 589832 | tf_op jit(solution)/shard_map/ppermute | solution.py:88
  91.1 2.2 %collective-permute-start.7 = (bf16[3,64,512]{2,1,0:T(8,128)(2,1)S(1)}, bf16[3,64,512]{2,1,0:T(8,128)(2,1)S(1)}, u32[]{:S(2)}, u32[]{:S(2)}) collective-permute-start(bf16[3,64,512]{2,1,0:T(8,128)(2,1)S(1)} %constant_dynamic-update-slice_fusion.4), channel_id=1, source_target_pairs={{0,128},{64,192},{128,0},{192,64},{1,129},{65,193},{129,1},{193,65... | collective-permute-start | bytes 589832 | tf_op jit(solution)/shard_map/ppermute | solution.py:88
  93.3 2.6 %collective-permute-start.8 = (bf16[3,64,512]{2,1,0:T(8,128)(2,1)S(1)}, bf16[3,64,512]{2,1,0:T(8,128)(2,1)S(1)}, u32[]{:S(2)}, u32[]{:S(2)}) collective-permute-start(bf16[3,64,512]{2,1,0:T(8,128)(2,1)S(1)} %constant_dynamic-update-slice_fusion.4), channel_id=1, source_target_pairs={{0,192},{64,0},{128,64},{192,128},{1,193},{65,1},{129,65},{193,129... | collective-permute-start | bytes 589832 | tf_op jit(solution)/shard_map/ppermute | solution.py:88
  96.0 3.4 %collective-permute-done.6 = bf16[3,64,512]{2,1,0:T(8,128)(2,1)S(1)} collective-permute-done((bf16[3,64,512]{2,1,0:T(8,128)(2,1)S(1)}, bf16[3,64,512]{2,1,0:T(8,128)(2,1)S(1)}, u32[]{:S(2)}, u32[]{:S(2)}) %collective-permute-start.6) | collective-permute-done | bytes 196640 | tf_op jit(solution)/shard_map/ppermute | solution.py:88
  99.4 2.9 %collective-permute-done.7 = bf16[3,64,512]{2,1,0:T(8,128)(2,1)S(1)} collective-permute-done((bf16[3,64,512]{2,1,0:T(8,128)(2,1)S(1)}, bf16[3,64,512]{2,1,0:T(8,128)(2,1)S(1)}, u32[]{:S(2)}, u32[]{:S(2)}) %collective-permute-start.7) | collective-permute-done | bytes 196640 | tf_op jit(solution)/shard_map/ppermute | solution.py:88
  102.4 2.8 %collective-permute-done.8 = bf16[3,64,512]{2,1,0:T(8,128)(2,1)S(1)} collective-permute-done((bf16[3,64,512]{2,1,0:T(8,128)(2,1)S(1)}, bf16[3,64,512]{2,1,0:T(8,128)(2,1)S(1)}, u32[]{:S(2)}, u32[]{:S(2)}) %collective-permute-start.8) | collective-permute-done | bytes 196640 | tf_op jit(solution)/shard_map/ppermute | solution.py:88
  112.5 4.9 %collective-permute-start.12 = (f32[128,512]{1,0:T(8,128)}, f32[128,512]{1,0:T(8,128)}, u32[]{:S(2)}, u32[]{:S(2)}) collective-permute-start(f32[128,512]{1,0:T(8,128)} %get-tuple-element.21), channel_id=1, source_target_pairs={{0,3},{1,0},{2,1},{3,2},{4,7},{5,4},{6,5},{7,6},{8,11},{9,8},{10,9... | collective-permute-start | bytes 786440 | tf_op jit(solution)/shard_map/ppermute | solution.py:77
  117.4 2.5 %collective-permute-start.11 = (f32[128,512]{1,0:T(8,128)}, f32[128,512]{1,0:T(8,128)}, u32[]{:S(2)}, u32[]{:S(2)}) collective-permute-start(f32[128,512]{1,0:T(8,128)} %get-tuple-element.22), channel_id=1, source_target_pairs={{0,2},{1,3},{2,0},{3,1},{4,6},{5,7},{6,4},{7,5},{8,10},{9,11},{10,... | collective-permute-start | bytes 786440 | tf_op jit(solution)/shard_map/ppermute | solution.py:77
  120.0 2.9 %collective-permute-start.10 = (f32[128,512]{1,0:T(8,128)S(1)}, f32[128,512]{1,0:T(8,128)}, u32[]{:S(2)}, u32[]{:S(2)}) collective-permute-start(f32[128,512]{1,0:T(8,128)S(1)} %get-tuple-element.20), channel_id=1, source_target_pairs={{0,1},{1,2},{2,3},{3,0},{4,5},{5,6},{6,7},{7,4},{8,9},{9,10},{10,1... | collective-permute-start | bytes 786440 | tf_op jit(solution)/shard_map/ppermute | solution.py:77
  131.6 3.6 %collective-permute-done.10 = f32[128,512]{1,0:T(8,128)} collective-permute-done((f32[128,512]{1,0:T(8,128)S(1)}, f32[128,512]{1,0:T(8,128)}, u32[]{:S(2)}, u32[]{:S(2)}) %collective-permute-start.10) | collective-permute-done | bytes 262176 | tf_op jit(solution)/shard_map/ppermute | solution.py:77
  136.4 10.3 %collective-permute-start.13 = (f32[64,512]{1,0:T(8,128)S(1)}, f32[64,512]{1,0:T(8,128)S(1)}, u32[]{:S(2)}, u32[]{:S(2)}) collective-permute-start(f32[64,512]{1,0:T(8,128)S(1)} %constant_dynamic-slice_fusion.2), channel_id=1, source_target_pairs={{0,4},{4,0},{1,5},{5,1},{2,6},{6,2},{3,7},{7,3},{8,12},{12,8},{9,1... | collective-permute-start | bytes 393224 | tf_op jit(solution)/shard_map/ppermute | solution.py:77
  147.3 3.1 %collective-permute-done.13 = f32[64,512]{1,0:T(8,128)S(1)} collective-permute-done((f32[64,512]{1,0:T(8,128)S(1)}, f32[64,512]{1,0:T(8,128)S(1)}, u32[]{:S(2)}, u32[]{:S(2)}) %collective-permute-start.13) | collective-permute-done | bytes 131104 | tf_op jit(solution)/shard_map/ppermute | solution.py:77
  153.3 4.3 %collective-permute-done.14 = f32[32,512]{1,0:T(8,128)S(1)} collective-permute-done((f32[32,512]{1,0:T(8,128)S(1)}, f32[32,512]{1,0:T(8,128)S(1)}, u32[]{:S(2)}, u32[]{:S(2)}) %collective-permute-start.14) | collective-permute-done | bytes 65568 | tf_op jit(solution)/shard_map/ppermute | solution.py:77
  157.6 6.6 %collective-permute-start.15 = (f32[16,512]{1,0:T(8,128)S(1)}, f32[16,512]{1,0:T(8,128)S(1)}, u32[]{:S(2)}, u32[]{:S(2)}) collective-permute-start(f32[16,512]{1,0:T(8,128)S(1)} %constant_dynamic-slice_fusion), channel_id=1, source_target_pairs={{0,16},{16,0},{1,17},{17,1},{2,18},{18,2},{3,19},{19,3},{4,20},{20... | collective-permute-start | bytes 98312 | tf_op jit(solution)/shard_map/ppermute | solution.py:77
  165.1 3.0 %copy.23 = bf16[256,2,16,32]{3,2,1,0:T(8,128)(2,1)S(1)} copy(bf16[256,2,16,32]{0,3,2,1:T(8,128)(2,1)S(1)} %divide_convert_fusion.2) | data formatting | bytes 1048576 | tf_op jit(solution)/shard_map/convert_element_type | solution.py:39
  168.1 2.8 %convert_element_type.34 = bf16[512,512]{1,0:T(8,128)(2,1)} reshape(bf16[256,2,16,32]{3,2,1,0:T(8,128)(2,1)S(1)} %copy.23) | data formatting | bytes 1048576 | tf_op jit(solution)/shard_map/convert_element_type | solution.py:39
  170.9 2.0 %copy.31 = bf16[512,512]{1,0:T(8,128)(2,1)} copy(bf16[512,512]{0,1:T(8,128)(2,1)} %bitcast.65) | data formatting | bytes 1048576
  172.9 3.0 %copy.26 = bf16[256,2,16,32]{3,2,1,0:T(8,128)(2,1)S(1)} copy(bf16[256,2,16,32]{0,3,2,1:T(8,128)(2,1)S(1)} %copy-done.3) | data formatting | bytes 1048576 | tf_op jit(solution)/shard_map/convert_element_type | solution.py:39
  175.9 2.8 %convert_element_type.36 = bf16[512,512]{1,0:T(8,128)(2,1)} reshape(bf16[256,2,16,32]{3,2,1,0:T(8,128)(2,1)S(1)} %copy.26) | data formatting | bytes 1048576 | tf_op jit(solution)/shard_map/convert_element_type | solution.py:39
  180.7 3.0 %copy.30 = bf16[256,2,16,32]{3,2,1,0:T(8,128)(2,1)S(1)} copy(bf16[256,2,16,32]{0,3,2,1:T(8,128)(2,1)S(1)} %copy-done.4) | data formatting | bytes 1048576 | tf_op jit(solution)/shard_map/convert_element_type | solution.py:39
  183.7 2.8 %convert_element_type.38 = bf16[512,512]{1,0:T(8,128)(2,1)} reshape(bf16[256,2,16,32]{3,2,1,0:T(8,128)(2,1)S(1)} %copy.30) | data formatting | bytes 1048576 | tf_op jit(solution)/shard_map/convert_element_type | solution.py:39
  (82 shorter events, 37.7 us)
Async XLA Ops:
  0.6 1.0 copy-start
  0.6 2.6 %copy-start.2 = (bf16[512,512]{1,0:T(8,128)(2,1)S(1)}, bf16[512,512]{1,0:T(8,128)(2,1)}, u32[]{:S(2)}) copy-start(bf16[512,512]{1,0:T(8,128)(2,1)} %param.5) | copy-start | bytes 1572868
  1.7 1.5 copy-start.6
  7.9 1.6 copy-start.1
  9.5 5.4 %collective-permute-start = (f32[3,256,512]{2,1,0:T(8,128)S(1)}, f32[3,256,512]{2,1,0:T(8,128)}, u32[]{:S(2)}, u32[]{:S(2)}) collective-permute-start(f32[3,256,512]{2,1,0:T(8,128)S(1)} %constant_dynamic-slice_fusion.10), channel_id=1, source_target_pairs={{0,32},{32,0},{1,33},{33,1},{2,34},{34,2},{3,35},{35,3},{4,36},{36... | collective-permute-start | bytes 4718600 | tf_op jit(solution)/shard_map/ppermute | solution.py:77
  18.0 17.4 %collective-permute-start.3 = (f32[3,64,512]{2,1,0:T(8,128)}, f32[3,64,512]{2,1,0:T(8,128)}, u32[]{:S(2)}, u32[]{:S(2)}) collective-permute-start(f32[3,64,512]{2,1,0:T(8,128)} %get-tuple-element.18), channel_id=1, source_target_pairs={{0,192},{64,0},{128,64},{192,128},{1,193},{65,1},{129,65},{193,129... | collective-permute-start | bytes 1179656 | tf_op jit(solution)/shard_map/ppermute | solution.py:77
  20.8 24.3 %collective-permute-start.2 = (f32[3,64,512]{2,1,0:T(8,128)S(1)}, f32[3,64,512]{2,1,0:T(8,128)}, u32[]{:S(2)}, u32[]{:S(2)}) collective-permute-start(f32[3,64,512]{2,1,0:T(8,128)S(1)} %get-tuple-element.19), channel_id=1, source_target_pairs={{0,128},{64,192},{128,0},{192,64},{1,129},{65,193},{129,1},{193,65... | collective-permute-start | bytes 1179656 | tf_op jit(solution)/shard_map/ppermute | solution.py:77
  29.1 17.1 %collective-permute-start.1 = (f32[3,64,512]{2,1,0:T(8,128)S(1)}, f32[3,64,512]{2,1,0:T(8,128)}, u32[]{:S(2)}, u32[]{:S(2)}) collective-permute-start(f32[3,64,512]{2,1,0:T(8,128)S(1)} %get-tuple-element.17), channel_id=1, source_target_pairs={{0,64},{64,128},{128,192},{192,0},{1,65},{65,129},{129,193},{193,1... | collective-permute-start | bytes 1179656 | tf_op jit(solution)/shard_map/ppermute | solution.py:77
  47.7 17.2 %collective-permute-start.4 = (f32[3,32,512]{2,1,0:T(8,128)S(1)}, f32[3,32,512]{2,1,0:T(8,128)S(1)}, u32[]{:S(2)}, u32[]{:S(2)}) collective-permute-start(f32[3,32,512]{2,1,0:T(8,128)S(1)} %constant_dynamic-slice_fusion.6), channel_id=1, source_target_pairs={{0,256},{256,0},{1,257},{257,1},{2,258},{258,2},{3,259},{259,3},{4... | collective-permute-start | bytes 589832 | tf_op jit(solution)/shard_map/ppermute | solution.py:77
  65.0 20.5 %collective-permute-start.5 = (bf16[3,32,512]{2,1,0:T(8,128)(2,1)S(1)}, bf16[3,32,512]{2,1,0:T(8,128)(2,1)S(1)}, u32[]{:S(2)}, u32[]{:S(2)}) collective-permute-start(bf16[3,32,512]{2,1,0:T(8,128)(2,1)S(1)} %pad_maximum_fusion.3), channel_id=1, source_target_pairs={{0,256},{256,0},{1,257},{257,1},{2,258},{258,2},{3,259},{259,3},{4... | collective-permute-start | bytes 294920 | tf_op jit(solution)/shard_map/ppermute | solution.py:88
  85.4 14.0 %collective-permute-start.6 = (bf16[3,64,512]{2,1,0:T(8,128)(2,1)S(1)}, bf16[3,64,512]{2,1,0:T(8,128)(2,1)S(1)}, u32[]{:S(2)}, u32[]{:S(2)}) collective-permute-start(bf16[3,64,512]{2,1,0:T(8,128)(2,1)S(1)} %constant_dynamic-update-slice_fusion.4), channel_id=1, source_target_pairs={{0,64},{64,128},{128,192},{192,0},{1,65},{65,129},{129,193},{193,1... | collective-permute-start | bytes 589832 | tf_op jit(solution)/shard_map/ppermute | solution.py:88
  91.1 17.2 %copy-start.5 = (bf16[512,512]{1,0:T(8,128)(2,1)S(1)}, bf16[512,512]{1,0:T(8,128)(2,1)}, u32[]{:S(2)}) copy-start(bf16[512,512]{1,0:T(8,128)(2,1)} %param.6) | copy-start | bytes 1572868
  91.1 11.3 %collective-permute-start.7 = (bf16[3,64,512]{2,1,0:T(8,128)(2,1)S(1)}, bf16[3,64,512]{2,1,0:T(8,128)(2,1)S(1)}, u32[]{:S(2)}, u32[]{:S(2)}) collective-permute-start(bf16[3,64,512]{2,1,0:T(8,128)(2,1)S(1)} %constant_dynamic-update-slice_fusion.4), channel_id=1, source_target_pairs={{0,128},{64,192},{128,0},{192,64},{1,129},{65,193},{129,1},{193,65... | collective-permute-start | bytes 589832 | tf_op jit(solution)/shard_map/ppermute | solution.py:88
  93.3 11.9 %collective-permute-start.8 = (bf16[3,64,512]{2,1,0:T(8,128)(2,1)S(1)}, bf16[3,64,512]{2,1,0:T(8,128)(2,1)S(1)}, u32[]{:S(2)}, u32[]{:S(2)}) collective-permute-start(bf16[3,64,512]{2,1,0:T(8,128)(2,1)S(1)} %constant_dynamic-update-slice_fusion.4), channel_id=1, source_target_pairs={{0,192},{64,0},{128,64},{192,128},{1,193},{65,1},{129,65},{193,129... | collective-permute-start | bytes 589832 | tf_op jit(solution)/shard_map/ppermute | solution.py:88
  105.3 4.2 %collective-permute-start.9 = (bf16[3,256,512]{2,1,0:T(8,128)(2,1)S(1)}, bf16[3,256,512]{2,1,0:T(8,128)(2,1)S(1)}, u32[]{:S(2)}, u32[]{:S(2)}) collective-permute-start(bf16[3,256,512]{2,1,0:T(8,128)(2,1)S(1)} %constant_dynamic-update-slice_fusion.1), channel_id=1, source_target_pairs={{0,32},{32,0},{1,33},{33,1},{2,34},{34,2},{3,35},{35,3},{4,36},{36... | collective-permute-start | bytes 2359304 | tf_op jit(solution)/shard_map/ppermute | solution.py:88
  110.0 1.0 copy-start.7
  112.5 19.1 %collective-permute-start.12 = (f32[128,512]{1,0:T(8,128)}, f32[128,512]{1,0:T(8,128)}, u32[]{:S(2)}, u32[]{:S(2)}) collective-permute-start(f32[128,512]{1,0:T(8,128)} %get-tuple-element.21), channel_id=1, source_target_pairs={{0,3},{1,0},{2,1},{3,2},{4,7},{5,4},{6,5},{7,6},{8,11},{9,8},{10,9... | collective-permute-start | bytes 786440 | tf_op jit(solution)/shard_map/ppermute | solution.py:77
  117.4 14.2 %collective-permute-start.11 = (f32[128,512]{1,0:T(8,128)}, f32[128,512]{1,0:T(8,128)}, u32[]{:S(2)}, u32[]{:S(2)}) collective-permute-start(f32[128,512]{1,0:T(8,128)} %get-tuple-element.22), channel_id=1, source_target_pairs={{0,2},{1,3},{2,0},{3,1},{4,6},{5,7},{6,4},{7,5},{8,10},{9,11},{10,... | collective-permute-start | bytes 786440 | tf_op jit(solution)/shard_map/ppermute | solution.py:77
  120.0 15.2 %collective-permute-start.10 = (f32[128,512]{1,0:T(8,128)S(1)}, f32[128,512]{1,0:T(8,128)}, u32[]{:S(2)}, u32[]{:S(2)}) collective-permute-start(f32[128,512]{1,0:T(8,128)S(1)} %get-tuple-element.20), channel_id=1, source_target_pairs={{0,1},{1,2},{2,3},{3,0},{4,5},{5,6},{6,7},{7,4},{8,9},{9,10},{10,1... | collective-permute-start | bytes 786440 | tf_op jit(solution)/shard_map/ppermute | solution.py:77
  125.3 2.3 %copy-start.9 = (bf16[512,512]{0,1:T(8,128)(2,1)S(1)}, bf16[512,512]{0,1:T(8,128)(2,1)}, u32[]{:S(2)}) copy-start(bf16[512,512]{0,1:T(8,128)(2,1)} %copy.21) | copy-start | bytes 1572868
  127.6 1.6 copy-start.11
  129.2 1.0 copy-start.8
  129.2 1.2 copy-start.10
  131.5 32.7 %copy-start.12 = (f32[256,16]{0,1:T(8,128)}, f32[256,16]{0,1:T(8,128)S(1)}, u32[]{:S(2)}) copy-start(f32[256,16]{0,1:T(8,128)S(1)} %get-tuple-element.36) | copy-start | bytes 49156
  136.4 14.0 %collective-permute-start.13 = (f32[64,512]{1,0:T(8,128)S(1)}, f32[64,512]{1,0:T(8,128)S(1)}, u32[]{:S(2)}, u32[]{:S(2)}) collective-permute-start(f32[64,512]{1,0:T(8,128)S(1)} %constant_dynamic-slice_fusion.2), channel_id=1, source_target_pairs={{0,4},{4,0},{1,5},{5,1},{2,6},{6,2},{3,7},{7,3},{8,12},{12,8},{9,1... | collective-permute-start | bytes 393224 | tf_op jit(solution)/shard_map/ppermute | solution.py:77
  150.4 7.1 %collective-permute-start.14 = (f32[32,512]{1,0:T(8,128)S(1)}, f32[32,512]{1,0:T(8,128)S(1)}, u32[]{:S(2)}, u32[]{:S(2)}) collective-permute-start(f32[32,512]{1,0:T(8,128)S(1)} %constant_dynamic-slice_fusion.1), channel_id=1, source_target_pairs={{0,8},{8,0},{1,9},{9,1},{2,10},{10,2},{3,11},{11,3},{4,12},{12,4},... | collective-permute-start | bytes 196616 | tf_op jit(solution)/shard_map/ppermute | solution.py:77
  157.6 28.9 %collective-permute-start.15 = (f32[16,512]{1,0:T(8,128)S(1)}, f32[16,512]{1,0:T(8,128)S(1)}, u32[]{:S(2)}, u32[]{:S(2)}) collective-permute-start(f32[16,512]{1,0:T(8,128)S(1)} %constant_dynamic-slice_fusion), channel_id=1, source_target_pairs={{0,16},{16,0},{1,17},{17,1},{2,18},{18,2},{3,19},{19,3},{4,20},{20... | collective-permute-start | bytes 98312 | tf_op jit(solution)/shard_map/ppermute | solution.py:77
  168.1 4.8 %copy-start.3 = (bf16[256,2,16,32]{0,3,2,1:T(8,128)(2,1)S(1)}, bf16[256,2,16,32]{0,3,2,1:T(8,128)(2,1)}, u32[]{:S(2)}) copy-start(bf16[256,2,16,32]{0,3,2,1:T(8,128)(2,1)} %divide_convert_fusion.1) | copy-start | bytes 1572868
  175.9 4.8 %copy-start.4 = (bf16[256,2,16,32]{0,3,2,1:T(8,128)(2,1)S(1)}, bf16[256,2,16,32]{0,3,2,1:T(8,128)(2,1)}, u32[]{:S(2)}) copy-start(bf16[256,2,16,32]{0,3,2,1:T(8,128)(2,1)} %divide_convert_fusion) | copy-start | bytes 1572868

commit v5 on v4

--- a/solution.py
+++ b/solution.py
@@ -21,14 +21,6 @@
     TENSOR = ("z4", "z2", "z1", "y2", "y1")
     TENSOR_STAGES = ("z1", "z2", "z4", "y1", "y2")
 FINE = PIPE + TENSOR
-
-
-def quantize_features(grad):
-    rows, cols = grad.shape
-    blocks = grad.reshape(rows // 32, 32, cols // 2, 2)
-    scales = jnp.max(jnp.abs(blocks), axis=(1, 3)) + 1e-06
-    mantissa = (blocks / scales[:, None, :, None]).reshape(grad.shape)
-    return (mantissa.astype(jnp.bfloat16), scales)
 
 
 def quantize_hidden(grad):
@@ -112,7 +104,7 @@
 
 
 def make_on_device(sizes):
-    def on_device(tokens, out_grad, w_gate, w_up, w_down):
+    def body(tokens, out_grad, w_gate, w_up, w_down):
         gate_part = jnp.dot(tokens, w_gate, preferred_element_type=jnp.float32)
         up_part = jnp.dot(tokens, w_up, preferred_element_type=jnp.float32)
         hidden_part = contract_last(out_grad, w_down)
@@ -133,7 +125,7 @@
             down_scales,
         )
 
-    return on_device
+    return body
 
 
 def fine_mesh(mesh):

time: 188 us -> 188 us (level)
  no operation moved by 1% of the time
where the time goes in v5:
time: 188 us; the launch traced here: 187 us
  starting transfers between devices  81.5 us (43%)
  waiting for transfers between devices  51.1 us (27%)
  local copies, waits for them, and re-layouts  34.5 us (18%)
  other arithmetic  10.5 us (6%)
  matrix products  8.12 us (4%)
    ppermute x11, starting transfers between devices, scatter_sum(): acc = acc + lax.ppermute(send, axis, perm=perm)  56.9 us
    ppermute x11, waiting for transfers between devices, scatter_sum(): acc = acc + lax.ppermute(send, axis, perm=perm)  33.8 us
    ppermute x5, starting transfers between devices, gather(): got = lax.ppermute(x, axis, perm=perm)  24.6 us
    ppermute x5, waiting for transfers between devices, gather(): got = lax.ppermute(x, axis, perm=perm)  17.3 us
    convert_element_type x6, local copies, waits for them, and re-layouts, quantize_hidden(): return (mantissa.astype(jnp.bfloat16), scales)  17.3 us
    unnamed x30, local copies, waits for them, and re-layouts  9.44 us
    dot_general x7, local copies, waits for them, and re-layouts, contract_first(): lax.dot_general(left, right, (((0,), (0,)), ((), ())), preferred_element_...  5.61 us
    add x7, other arithmetic, scatter_sum(): acc = acc + lax.ppermute(send, axis, perm=perm)  5.47 us
  transfers between devices with their start and end apart: 16, of which 12 were waited for; matrix products, arithmetic and copies ran while one was open for 18% of the time, Pallas kernels for 0%

profile of v5, /device:TPU:6, one launch (start us, length us, event | category | flops | bytes accessed | tf_op | source)
XLA Modules:
  0.0 187.1 jit_solution(10675825795903025155)
XLA Ops:
  3.7 2.7 %convolution_bitcast_fusion = f32[1,512,512]{2,1,0:T(8,128)} fusion(bf16[512,512]{1,0:T(8,128)(2,1)} %param.6, bf16[512,512]{1,0:T(8,128)(2,1)} %param.9), kind=kOutput, calls=%fused_computation.4 | convolution fusion | flops 268435456 | bytes 2097152 | tf_op jit(solution)/shard_map/dot_general | solution.py:39
  11.5 3.5 %collective-permute-done = f32[3,256,512]{2,1,0:T(8,128)} collective-permute-done((f32[3,256,512]{2,1,0:T(8,128)S(1)}, f32[3,256,512]{2,1,0:T(8,128)}, u32[]{:S(2)}, u32[]{:S(2)}) %collective-permute-start) | collective-permute-done | bytes 1572896 | tf_op jit(solution)/shard_map/ppermute | solution.py:69
  14.9 2.2 %dynamic-slice_add_fusion = f32[3,256,512]{2,1,0:T(8,128)S(1)} fusion(f32[3,256,512]{2,1,0:T(8,128)} %collective-permute-done, f32[3,512,512]{2,1,0:T(8,128)} %copy-done.1, s32[]{:T(128)S(6)} %select_n.136), kind=kLoop, calls=%fused_computation.2 | loop fusion | flops 393216 | bytes 4718596 | tf_op jit(solution)/shard_map/add | solution.py:69
  18.0 2.7 %collective-permute-start.3 = (f32[3,64,512]{2,1,0:T(8,128)}, f32[3,64,512]{2,1,0:T(8,128)}, u32[]{:S(2)}, u32[]{:S(2)}) collective-permute-start(f32[3,64,512]{2,1,0:T(8,128)} %get-tuple-element.18), channel_id=1, source_target_pairs={{0,192},{64,0},{128,64},{192,128},{1,193},{65,1},{129,65},{193,129... | collective-permute-start | bytes 1179656 | tf_op jit(solution)/shard_map/ppermute | solution.py:69
  20.8 8.4 %collective-permute-start.2 = (f32[3,64,512]{2,1,0:T(8,128)S(1)}, f32[3,64,512]{2,1,0:T(8,128)}, u32[]{:S(2)}, u32[]{:S(2)}) collective-permute-start(f32[3,64,512]{2,1,0:T(8,128)S(1)} %get-tuple-element.19), channel_id=1, source_target_pairs={{0,128},{64,192},{128,0},{192,64},{1,129},{65,193},{129,1},{193,65... | collective-permute-start | bytes 1179656 | tf_op jit(solution)/shard_map/ppermute | solution.py:69
  31.1 4.4 %collective-permute-done.3 = f32[3,64,512]{2,1,0:T(8,128)} collective-permute-done((f32[3,64,512]{2,1,0:T(8,128)}, f32[3,64,512]{2,1,0:T(8,128)}, u32[]{:S(2)}, u32[]{:S(2)}) %collective-permute-start.3) | collective-permute-done | bytes 393248 | tf_op jit(solution)/shard_map/ppermute | solution.py:69
  35.5 9.6 %collective-permute-done.2 = f32[3,64,512]{2,1,0:T(8,128)} collective-permute-done((f32[3,64,512]{2,1,0:T(8,128)S(1)}, f32[3,64,512]{2,1,0:T(8,128)}, u32[]{:S(2)}, u32[]{:S(2)}) %collective-permute-start.2) | collective-permute-done | bytes 393248 | tf_op jit(solution)/shard_map/ppermute | solution.py:69
  47.7 12.8 %collective-permute-start.4 = (f32[3,32,512]{2,1,0:T(8,128)S(1)}, f32[3,32,512]{2,1,0:T(8,128)S(1)}, u32[]{:S(2)}, u32[]{:S(2)}) collective-permute-start(f32[3,32,512]{2,1,0:T(8,128)S(1)} %constant_dynamic-slice_fusion.6), channel_id=1, source_target_pairs={{0,256},{256,0},{1,257},{257,1},{2,258},{258,2},{3,259},{259,3},{4... | collective-permute-start | bytes 589832 | tf_op jit(solution)/shard_map/ppermute | solution.py:69
  60.5 4.3 %collective-permute-done.4 = f32[3,32,512]{2,1,0:T(8,128)S(1)} collective-permute-done((f32[3,32,512]{2,1,0:T(8,128)S(1)}, f32[3,32,512]{2,1,0:T(8,128)S(1)}, u32[]{:S(2)}, u32[]{:S(2)}) %collective-permute-start.4) | collective-permute-done | bytes 196640 | tf_op jit(solution)/shard_map/ppermute | solution.py:69
  65.0 12.3 %collective-permute-start.5 = (bf16[3,32,512]{2,1,0:T(8,128)(2,1)S(1)}, bf16[3,32,512]{2,1,0:T(8,128)(2,1)S(1)}, u32[]{:S(2)}, u32[]{:S(2)}) collective-permute-start(bf16[3,32,512]{2,1,0:T(8,128)(2,1)S(1)} %pad_maximum_fusion.3), channel_id=1, source_target_pairs={{0,256},{256,0},{1,257},{257,1},{2,258},{258,2},{3,259},{259,3},{4... | collective-permute-start | bytes 294920 | tf_op jit(solution)/shard_map/ppermute | solution.py:80
  77.3 8.1 %collective-permute-done.5 = bf16[3,32,512]{2,1,0:T(8,128)(2,1)S(1)} collective-permute-done((bf16[3,32,512]{2,1,0:T(8,128)(2,1)S(1)}, bf16[3,32,512]{2,1,0:T(8,128)(2,1)S(1)}, u32[]{:S(2)}, u32[]{:S(2)}) %collective-permute-start.5) | collective-permute-done | bytes 98336 | tf_op jit(solution)/shard_map/ppermute | solution.py:80
  85.4 5.6 %collective-permute-start.6 = (bf16[3,64,512]{2,1,0:T(8,128)(2,1)S(1)}, bf16[3,64,512]{2,1,0:T(8,128)(2,1)S(1)}, u32[]{:S(2)}, u32[]{:S(2)}) collective-permute-start(bf16[3,64,512]{2,1,0:T(8,128)(2,1)S(1)} %constant_dynamic-update-slice_fusion.4), channel_id=1, source_target_pairs={{0,64},{64,128},{128,192},{192,0},{1,65},{65,129},{129,193},{193,1... | collective-permute-start | bytes 589832 | tf_op jit(solution)/shard_map/ppermute | solution.py:80
  91.1 2.2 %collective-permute-start.7 = (bf16[3,64,512]{2,1,0:T(8,128)(2,1)S(1)}, bf16[3,64,512]{2,1,0:T(8,128)(2,1)S(1)}, u32[]{:S(2)}, u32[]{:S(2)}) collective-permute-start(bf16[3,64,512]{2,1,0:T(8,128)(2,1)S(1)} %constant_dynamic-update-slice_fusion.4), channel_id=1, source_target_pairs={{0,128},{64,192},{128,0},{192,64},{1,129},{65,193},{129,1},{193,65... | collective-permute-start | bytes 589832 | tf_op jit(solution)/shard_map/ppermute | solution.py:80
  93.3 2.6 %collective-permute-start.8 = (bf16[3,64,512]{2,1,0:T(8,128)(2,1)S(1)}, bf16[3,64,512]{2,1,0:T(8,128)(2,1)S(1)}, u32[]{:S(2)}, u32[]{:S(2)}) collective-permute-start(bf16[3,64,512]{2,1,0:T(8,128)(2,1)S(1)} %constant_dynamic-update-slice_fusion.4), channel_id=1, source_target_pairs={{0,192},{64,0},{128,64},{192,128},{1,193},{65,1},{129,65},{193,129... | collective-permute-start | bytes 589832 | tf_op jit(solution)/shard_map/ppermute | solution.py:80
  96.0 3.4 %collective-permute-done.6 = bf16[3,64,512]{2,1,0:T(8,128)(2,1)S(1)} collective-permute-done((bf16[3,64,512]{2,1,0:T(8,128)(2,1)S(1)}, bf16[3,64,512]{2,1,0:T(8,128)(2,1)S(1)}, u32[]{:S(2)}, u32[]{:S(2)}) %collective-permute-start.6) | collective-permute-done | bytes 196640 | tf_op jit(solution)/shard_map/ppermute | solution.py:80
  99.4 2.9 %collective-permute-done.7 = bf16[3,64,512]{2,1,0:T(8,128)(2,1)S(1)} collective-permute-done((bf16[3,64,512]{2,1,0:T(8,128)(2,1)S(1)}, bf16[3,64,512]{2,1,0:T(8,128)(2,1)S(1)}, u32[]{:S(2)}, u32[]{:S(2)}) %collective-permute-start.7) | collective-permute-done | bytes 196640 | tf_op jit(solution)/shard_map/ppermute | solution.py:80
  102.4 2.8 %collective-permute-done.8 = bf16[3,64,512]{2,1,0:T(8,128)(2,1)S(1)} collective-permute-done((bf16[3,64,512]{2,1,0:T(8,128)(2,1)S(1)}, bf16[3,64,512]{2,1,0:T(8,128)(2,1)S(1)}, u32[]{:S(2)}, u32[]{:S(2)}) %collective-permute-start.8) | collective-permute-done | bytes 196640 | tf_op jit(solution)/shard_map/ppermute | solution.py:80
  112.5 4.9 %collective-permute-start.12 = (f32[128,512]{1,0:T(8,128)}, f32[128,512]{1,0:T(8,128)}, u32[]{:S(2)}, u32[]{:S(2)}) collective-permute-start(f32[128,512]{1,0:T(8,128)} %get-tuple-element.21), channel_id=1, source_target_pairs={{0,3},{1,0},{2,1},{3,2},{4,7},{5,4},{6,5},{7,6},{8,11},{9,8},{10,9... | collective-permute-start | bytes 786440 | tf_op jit(solution)/shard_map/ppermute | solution.py:69
  117.4 2.5 %collective-permute-start.11 = (f32[128,512]{1,0:T(8,128)}, f32[128,512]{1,0:T(8,128)}, u32[]{:S(2)}, u32[]{:S(2)}) collective-permute-start(f32[128,512]{1,0:T(8,128)} %get-tuple-element.22), channel_id=1, source_target_pairs={{0,2},{1,3},{2,0},{3,1},{4,6},{5,7},{6,4},{7,5},{8,10},{9,11},{10,... | collective-permute-start | bytes 786440 | tf_op jit(solution)/shard_map/ppermute | solution.py:69
  120.0 2.9 %collective-permute-start.10 = (f32[128,512]{1,0:T(8,128)S(1)}, f32[128,512]{1,0:T(8,128)}, u32[]{:S(2)}, u32[]{:S(2)}) collective-permute-start(f32[128,512]{1,0:T(8,128)S(1)} %get-tuple-element.20), channel_id=1, source_target_pairs={{0,1},{1,2},{2,3},{3,0},{4,5},{5,6},{6,7},{7,4},{8,9},{9,10},{10,1... | collective-permute-start | bytes 786440 | tf_op jit(solution)/shard_map/ppermute | solution.py:69
  131.6 3.6 %collective-permute-done.10 = f32[128,512]{1,0:T(8,128)} collective-permute-done((f32[128,512]{1,0:T(8,128)S(1)}, f32[128,512]{1,0:T(8,128)}, u32[]{:S(2)}, u32[]{:S(2)}) %collective-permute-start.10) | collective-permute-done | bytes 262176 | tf_op jit(solution)/shard_map/ppermute | solution.py:69
  136.4 10.3 %collective-permute-start.13 = (f32[64,512]{1,0:T(8,128)S(1)}, f32[64,512]{1,0:T(8,128)S(1)}, u32[]{:S(2)}, u32[]{:S(2)}) collective-permute-start(f32[64,512]{1,0:T(8,128)S(1)} %constant_dynamic-slice_fusion.2), channel_id=1, source_target_pairs={{0,4},{4,0},{1,5},{5,1},{2,6},{6,2},{3,7},{7,3},{8,12},{12,8},{9,1... | collective-permute-start | bytes 393224 | tf_op jit(solution)/shard_map/ppermute | solution.py:69
  147.3 3.1 %collective-permute-done.13 = f32[64,512]{1,0:T(8,128)S(1)} collective-permute-done((f32[64,512]{1,0:T(8,128)S(1)}, f32[64,512]{1,0:T(8,128)S(1)}, u32[]{:S(2)}, u32[]{:S(2)}) %collective-permute-start.13) | collective-permute-done | bytes 131104 | tf_op jit(solution)/shard_map/ppermute | solution.py:69
  153.3 4.3 %collective-permute-done.14 = f32[32,512]{1,0:T(8,128)S(1)} collective-permute-done((f32[32,512]{1,0:T(8,128)S(1)}, f32[32,512]{1,0:T(8,128)S(1)}, u32[]{:S(2)}, u32[]{:S(2)}) %collective-permute-start.14) | collective-permute-done | bytes 65568 | tf_op jit(solution)/shard_map/ppermute | solution.py:69
  157.6 6.6 %collective-permute-start.15 = (f32[16,512]{1,0:T(8,128)S(1)}, f32[16,512]{1,0:T(8,128)S(1)}, u32[]{:S(2)}, u32[]{:S(2)}) collective-permute-start(f32[16,512]{1,0:T(8,128)S(1)} %constant_dynamic-slice_fusion), channel_id=1, source_target_pairs={{0,16},{16,0},{1,17},{17,1},{2,18},{18,2},{3,19},{19,3},{4,20},{20... | collective-permute-start | bytes 98312 | tf_op jit(solution)/shard_map/ppermute | solution.py:69
  165.1 3.0 %copy.23 = bf16[256,2,16,32]{3,2,1,0:T(8,128)(2,1)S(1)} copy(bf16[256,2,16,32]{0,3,2,1:T(8,128)(2,1)S(1)} %divide_convert_fusion.2) | data formatting | bytes 1048576 | tf_op jit(solution)/shard_map/convert_element_type | solution.py:31
  168.1 2.8 %convert_element_type.34 = bf16[512,512]{1,0:T(8,128)(2,1)} reshape(bf16[256,2,16,32]{3,2,1,0:T(8,128)(2,1)S(1)} %copy.23) | data formatting | bytes 1048576 | tf_op jit(solution)/shard_map/convert_element_type | solution.py:31
  170.9 2.0 %copy.31 = bf16[512,512]{1,0:T(8,128)(2,1)} copy(bf16[512,512]{0,1:T(8,128)(2,1)} %bitcast.65) | data formatting | bytes 1048576
  172.9 3.0 %copy.26 = bf16[256,2,16,32]{3,2,1,0:T(8,128)(2,1)S(1)} copy(bf16[256,2,16,32]{0,3,2,1:T(8,128)(2,1)S(1)} %copy-done.3) | data formatting | bytes 1048576 | tf_op jit(solution)/shard_map/convert_element_type | solution.py:31
  175.9 2.8 %convert_element_type.36 = bf16[512,512]{1,0:T(8,128)(2,1)} reshape(bf16[256,2,16,32]{3,2,1,0:T(8,128)(2,1)S(1)} %copy.26) | data formatting | bytes 1048576 | tf_op jit(solution)/shard_map/convert_element_type | solution.py:31
  180.7 3.0 %copy.30 = bf16[256,2,16,32]{3,2,1,0:T(8,128)(2,1)S(1)} copy(bf16[256,2,16,32]{0,3,2,1:T(8,128)(2,1)S(1)} %copy-done.4) | data formatting | bytes 1048576 | tf_op jit(solution)/shard_map/convert_element_type | solution.py:31
  183.7 2.8 %convert_element_type.38 = bf16[512,512]{1,0:T(8,128)(2,1)} reshape(bf16[256,2,16,32]{3,2,1,0:T(8,128)(2,1)S(1)} %copy.30) | data formatting | bytes 1048576 | tf_op jit(solution)/shard_map/convert_element_type | solution.py:31
  (82 shorter events, 37.7 us)
Async XLA Ops:
  0.6 1.0 copy-start
  0.6 2.6 %copy-start.2 = (bf16[512,512]{1,0:T(8,128)(2,1)S(1)}, bf16[512,512]{1,0:T(8,128)(2,1)}, u32[]{:S(2)}) copy-start(bf16[512,512]{1,0:T(8,128)(2,1)} %param.5) | copy-start | bytes 1572868
  1.7 1.5 copy-start.6
  7.9 1.6 copy-start.1
  9.5 5.4 %collective-permute-start = (f32[3,256,512]{2,1,0:T(8,128)S(1)}, f32[3,256,512]{2,1,0:T(8,128)}, u32[]{:S(2)}, u32[]{:S(2)}) collective-permute-start(f32[3,256,512]{2,1,0:T(8,128)S(1)} %constant_dynamic-slice_fusion.10), channel_id=1, source_target_pairs={{0,32},{32,0},{1,33},{33,1},{2,34},{34,2},{3,35},{35,3},{4,36},{36... | collective-permute-start | bytes 4718600 | tf_op jit(solution)/shard_map/ppermute | solution.py:69
  18.0 17.4 %collective-permute-start.3 = (f32[3,64,512]{2,1,0:T(8,128)}, f32[3,64,512]{2,1,0:T(8,128)}, u32[]{:S(2)}, u32[]{:S(2)}) collective-permute-start(f32[3,64,512]{2,1,0:T(8,128)} %get-tuple-element.18), channel_id=1, source_target_pairs={{0,192},{64,0},{128,64},{192,128},{1,193},{65,1},{129,65},{193,129... | collective-permute-start | bytes 1179656 | tf_op jit(solution)/shard_map/ppermute | solution.py:69
  20.8 24.3 %collective-permute-start.2 = (f32[3,64,512]{2,1,0:T(8,128)S(1)}, f32[3,64,512]{2,1,0:T(8,128)}, u32[]{:S(2)}, u32[]{:S(2)}) collective-permute-start(f32[3,64,512]{2,1,0:T(8,128)S(1)} %get-tuple-element.19), channel_id=1, source_target_pairs={{0,128},{64,192},{128,0},{192,64},{1,129},{65,193},{129,1},{193,65... | collective-permute-start | bytes 1179656 | tf_op jit(solution)/shard_map/ppermute | solution.py:69
  29.1 17.1 %collective-permute-start.1 = (f32[3,64,512]{2,1,0:T(8,128)S(1)}, f32[3,64,512]{2,1,0:T(8,128)}, u32[]{:S(2)}, u32[]{:S(2)}) collective-permute-start(f32[3,64,512]{2,1,0:T(8,128)S(1)} %get-tuple-element.17), channel_id=1, source_target_pairs={{0,64},{64,128},{128,192},{192,0},{1,65},{65,129},{129,193},{193,1... | collective-permute-start | bytes 1179656 | tf_op jit(solution)/shard_map/ppermute | solution.py:69
  47.7 17.2 %collective-permute-start.4 = (f32[3,32,512]{2,1,0:T(8,128)S(1)}, f32[3,32,512]{2,1,0:T(8,128)S(1)}, u32[]{:S(2)}, u32[]{:S(2)}) collective-permute-start(f32[3,32,512]{2,1,0:T(8,128)S(1)} %constant_dynamic-slice_fusion.6), channel_id=1, source_target_pairs={{0,256},{256,0},{1,257},{257,1},{2,258},{258,2},{3,259},{259,3},{4... | collective-permute-start | bytes 589832 | tf_op jit(solution)/shard_map/ppermute | solution.py:69
  65.0 20.5 %collective-permute-start.5 = (bf16[3,32,512]{2,1,0:T(8,128)(2,1)S(1)}, bf16[3,32,512]{2,1,0:T(8,128)(2,1)S(1)}, u32[]{:S(2)}, u32[]{:S(2)}) collective-permute-start(bf16[3,32,512]{2,1,0:T(8,128)(2,1)S(1)} %pad_maximum_fusion.3), channel_id=1, source_target_pairs={{0,256},{256,0},{1,257},{257,1},{2,258},{258,2},{3,259},{259,3},{4... | collective-permute-start | bytes 294920 | tf_op jit(solution)/shard_map/ppermute | solution.py:80
  85.4 14.0 %collective-permute-start.6 = (bf16[3,64,512]{2,1,0:T(8,128)(2,1)S(1)}, bf16[3,64,512]{2,1,0:T(8,128)(2,1)S(1)}, u32[]{:S(2)}, u32[]{:S(2)}) collective-permute-start(bf16[3,64,512]{2,1,0:T(8,128)(2,1)S(1)} %constant_dynamic-update-slice_fusion.4), channel_id=1, source_target_pairs={{0,64},{64,128},{128,192},{192,0},{1,65},{65,129},{129,193},{193,1... | collective-permute-start | bytes 589832 | tf_op jit(solution)/shard_map/ppermute | solution.py:80
  91.1 17.2 %copy-start.5 = (bf16[512,512]{1,0:T(8,128)(2,1)S(1)}, bf16[512,512]{1,0:T(8,128)(2,1)}, u32[]{:S(2)}) copy-start(bf16[512,512]{1,0:T(8,128)(2,1)} %param.6) | copy-start | bytes 1572868
  91.1 11.3 %collective-permute-start.7 = (bf16[3,64,512]{2,1,0:T(8,128)(2,1)S(1)}, bf16[3,64,512]{2,1,0:T(8,128)(2,1)S(1)}, u32[]{:S(2)}, u32[]{:S(2)}) collective-permute-start(bf16[3,64,512]{2,1,0:T(8,128)(2,1)S(1)} %constant_dynamic-update-slice_fusion.4), channel_id=1, source_target_pairs={{0,128},{64,192},{128,0},{192,64},{1,129},{65,193},{129,1},{193,65... | collective-permute-start | bytes 589832 | tf_op jit(solution)/shard_map/ppermute | solution.py:80
  93.3 11.9 %collective-permute-start.8 = (bf16[3,64,512]{2,1,0:T(8,128)(2,1)S(1)}, bf16[3,64,512]{2,1,0:T(8,128)(2,1)S(1)}, u32[]{:S(2)}, u32[]{:S(2)}) collective-permute-start(bf16[3,64,512]{2,1,0:T(8,128)(2,1)S(1)} %constant_dynamic-update-slice_fusion.4), channel_id=1, source_target_pairs={{0,192},{64,0},{128,64},{192,128},{1,193},{65,1},{129,65},{193,129... | collective-permute-start | bytes 589832 | tf_op jit(solution)/shard_map/ppermute | solution.py:80
  105.3 4.2 %collective-permute-start.9 = (bf16[3,256,512]{2,1,0:T(8,128)(2,1)S(1)}, bf16[3,256,512]{2,1,0:T(8,128)(2,1)S(1)}, u32[]{:S(2)}, u32[]{:S(2)}) collective-permute-start(bf16[3,256,512]{2,1,0:T(8,128)(2,1)S(1)} %constant_dynamic-update-slice_fusion.1), channel_id=1, source_target_pairs={{0,32},{32,0},{1,33},{33,1},{2,34},{34,2},{3,35},{35,3},{4,36},{36... | collective-permute-start | bytes 2359304 | tf_op jit(solution)/shard_map/ppermute | solution.py:80
  110.0 1.0 copy-start.7
  112.5 19.1 %collective-permute-start.12 = (f32[128,512]{1,0:T(8,128)}, f32[128,512]{1,0:T(8,128)}, u32[]{:S(2)}, u32[]{:S(2)}) collective-permute-start(f32[128,512]{1,0:T(8,128)} %get-tuple-element.21), channel_id=1, source_target_pairs={{0,3},{1,0},{2,1},{3,2},{4,7},{5,4},{6,5},{7,6},{8,11},{9,8},{10,9... | collective-permute-start | bytes 786440 | tf_op jit(solution)/shard_map/ppermute | solution.py:69
  117.4 14.2 %collective-permute-start.11 = (f32[128,512]{1,0:T(8,128)}, f32[128,512]{1,0:T(8,128)}, u32[]{:S(2)}, u32[]{:S(2)}) collective-permute-start(f32[128,512]{1,0:T(8,128)} %get-tuple-element.22), channel_id=1, source_target_pairs={{0,2},{1,3},{2,0},{3,1},{4,6},{5,7},{6,4},{7,5},{8,10},{9,11},{10,... | collective-permute-start | bytes 786440 | tf_op jit(solution)/shard_map/ppermute | solution.py:69
  120.0 15.2 %collective-permute-start.10 = (f32[128,512]{1,0:T(8,128)S(1)}, f32[128,512]{1,0:T(8,128)}, u32[]{:S(2)}, u32[]{:S(2)}) collective-permute-start(f32[128,512]{1,0:T(8,128)S(1)} %get-tuple-element.20), channel_id=1, source_target_pairs={{0,1},{1,2},{2,3},{3,0},{4,5},{5,6},{6,7},{7,4},{8,9},{9,10},{10,1... | collective-permute-start | bytes 786440 | tf_op jit(solution)/shard_map/ppermute | solution.py:69
  125.3 2.3 %copy-start.9 = (bf16[512,512]{0,1:T(8,128)(2,1)S(1)}, bf16[512,512]{0,1:T(8,128)(2,1)}, u32[]{:S(2)}) copy-start(bf16[512,512]{0,1:T(8,128)(2,1)} %copy.21) | copy-start | bytes 1572868
  127.6 1.6 copy-start.11
  129.2 1.0 copy-start.8
  129.2 1.2 copy-start.10
  131.5 32.7 %copy-start.12 = (f32[256,16]{0,1:T(8,128)}, f32[256,16]{0,1:T(8,128)S(1)}, u32[]{:S(2)}) copy-start(f32[256,16]{0,1:T(8,128)S(1)} %get-tuple-element.36) | copy-start | bytes 49156
  136.4 14.0 %collective-permute-start.13 = (f32[64,512]{1,0:T(8,128)S(1)}, f32[64,512]{1,0:T(8,128)S(1)}, u32[]{:S(2)}, u32[]{:S(2)}) collective-permute-start(f32[64,512]{1,0:T(8,128)S(1)} %constant_dynamic-slice_fusion.2), channel_id=1, source_target_pairs={{0,4},{4,0},{1,5},{5,1},{2,6},{6,2},{3,7},{7,3},{8,12},{12,8},{9,1... | collective-permute-start | bytes 393224 | tf_op jit(solution)/shard_map/ppermute | solution.py:69
  150.4 7.1 %collective-permute-start.14 = (f32[32,512]{1,0:T(8,128)S(1)}, f32[32,512]{1,0:T(8,128)S(1)}, u32[]{:S(2)}, u32[]{:S(2)}) collective-permute-start(f32[32,512]{1,0:T(8,128)S(1)} %constant_dynamic-slice_fusion.1), channel_id=1, source_target_pairs={{0,8},{8,0},{1,9},{9,1},{2,10},{10,2},{3,11},{11,3},{4,12},{12,4},... | collective-permute-start | bytes 196616 | tf_op jit(solution)/shard_map/ppermute | solution.py:69
  157.6 28.9 %collective-permute-start.15 = (f32[16,512]{1,0:T(8,128)S(1)}, f32[16,512]{1,0:T(8,128)S(1)}, u32[]{:S(2)}, u32[]{:S(2)}) collective-permute-start(f32[16,512]{1,0:T(8,128)S(1)} %constant_dynamic-slice_fusion), channel_id=1, source_target_pairs={{0,16},{16,0},{1,17},{17,1},{2,18},{18,2},{3,19},{19,3},{4,20},{20... | collective-permute-start | bytes 98312 | tf_op jit(solution)/shard_map/ppermute | solution.py:69
  168.1 4.8 %copy-start.3 = (bf16[256,2,16,32]{0,3,2,1:T(8,128)(2,1)S(1)}, bf16[256,2,16,32]{0,3,2,1:T(8,128)(2,1)}, u32[]{:S(2)}) copy-start(bf16[256,2,16,32]{0,3,2,1:T(8,128)(2,1)} %divide_convert_fusion.1) | copy-start | bytes 1572868
  175.9 4.8 %copy-start.4 = (bf16[256,2,16,32]{0,3,2,1:T(8,128)(2,1)S(1)}, bf16[256,2,16,32]{0,3,2,1:T(8,128)(2,1)}, u32[]{:S(2)}) copy-start(bf16[256,2,16,32]{0,3,2,1:T(8,128)(2,1)} %divide_convert_fusion) | copy-start | bytes 1572868
